TPU v7x, 256 devices: a whole 4x4x8 slice. The times are simulated.
256 devices in a mesh: req: 32 (over x, y, core), kv: 8 (over z).
Axes of the slice: x: 4, y: 4, z: 8, core: 2. Of those that a mesh axis runs over, the one named last changes fastest.
Arguments:
- hidden: bfloat16 [512, 1536], P('req'), may hold values from -6 to 6
- norm_gain: float32 [1536], replicated, may hold values from 0.5 to 1.5
- w_qkv: bfloat16 [1536, 3072], P(None, 'kv'), may hold values from -0.15625 to 0.15625
- w_out: bfloat16 [1536, 1536], P(None, 'kv'), may hold values from -0.15625 to 0.15625
- cache_pages: bfloat16 [6144, 2, 8, 96, 128], P('req', None, 'kv'), may hold values from -340 to 340
- lengths: int32 [512], P('req'), may hold values from 1 to 16384, as said below
- page_table: int32 [512, 128], P('req'), may hold values from 0 to 191, as said below
- occupant: int32 [512], replicated, may hold values from 0 to 511, each once
Outputs:
- mixed: bfloat16 [512, 1536], P('req', 'kv')
Inputs may be any that keep to these rules, and one draw needn't show every extreme that they name: `occupant`: every request is served at exactly one slot. Slot s holds ceil(lengths[s] / 128) pages; on every index of req the pages of its 16 slots fit its pool of 192, some pool is full, and some request has 16384 tokens. `page_table`: the first ceil(lengths[s] / 128) entries of slot s are pages of its own pool that no other slot of that pool uses; later entries are arbitrary pages of the pool.
All inputs are finite; a program needn't handle non-finite values.
Results may differ from a plain program's by a relative error of at most 0.0043.
Values may be sent and summed in bfloat16 or wider, within the bound.
No kernel may reach another device: no remote copies, remote signals or barrier semaphores. Data moves between devices by JAX's collectives and lax.ppermute only.
A program may use at most 64 MiB of HBM per device.

v0:
```python
import math

import jax
import jax.numpy as jnp
from jax import lax
from jax.sharding import PartitionSpec as P

HD = 96
PAGE = 128
MAXP = 128
GROUP = 2


def per_device(hidden, norm_gain, w_qkv, w_out, cache_pages, lengths, page_table, occupant):
    slot_count = hidden.shape[0]
    pool_size = cache_pages.shape[0]
    kv_local = cache_pages.shape[2]
    first_slot = lax.axis_index("req") * slot_count
    hidden_wide = hidden.astype(jnp.float32)
    normed = (
        hidden_wide
        * lax.rsqrt(jnp.mean(hidden_wide * hidden_wide, axis=1, keepdims=True) + 1e-05)
        * norm_gain
    ).astype(jnp.bfloat16)
    served = lax.dynamic_slice_in_dim(occupant, first_slot, slot_count)
    every_normed = lax.all_gather(normed, "req", axis=0, tiled=True)
    picked = jnp.take(every_normed, served, axis=0)
    slot_rows = jnp.dot(picked, w_qkv, preferred_element_type=jnp.float32).astype(jnp.bfloat16)
    slot_rows = slot_rows.reshape(slot_count, kv_local, GROUP + 2, HD)
    queries = slot_rows[:, :, :GROUP]
    own_key = slot_rows[:, :, GROUP]
    own_value = slot_rows[:, :, GROUP + 1]
    score_scale = 1.0 / math.sqrt(HD)
    pages_used = (lengths + PAGE - 1) // PAGE
    live_page = jnp.arange(MAXP, dtype=jnp.int32)[None, :] < pages_used[:, None]
    matches = (
        (page_table[:, :, None] == jnp.arange(pool_size, dtype=jnp.int32)[None, None, :])
        & live_page[:, :, None]
    ).astype(jnp.int32)
    owner_table = jnp.sum(matches, axis=1)
    slot_ids = jnp.arange(slot_count, dtype=jnp.int32)
    page_owner = jnp.sum(owner_table * slot_ids[:, None], axis=0)
    page_rank = jnp.sum(matches * jnp.arange(MAXP, dtype=jnp.int32)[None, :, None], axis=(0, 1))
    page_limit = jnp.sum(owner_table * lengths[:, None], axis=0)
    offsets = page_rank[:, None] * PAGE + jnp.arange(PAGE, dtype=jnp.int32)[None, :]
    token_live = offsets < page_limit[:, None]
    page_queries = jnp.take(queries, page_owner, axis=0)
    scores = (
        jnp.einsum(
            "pgjd,pgdt->pgjt", page_queries, cache_pages[:, 0], preferred_element_type=jnp.float32
        )
        * score_scale
    )
    scores = jnp.where(token_live[:, None, None, :], scores, -jnp.inf)
    page_max = jnp.max(scores, axis=-1)
    own_score = (
        jnp.sum(queries.astype(jnp.float32) * own_key.astype(jnp.float32)[:, :, None, :], axis=-1)
        * score_scale
    )
    owner_mask = owner_table > 0
    slot_max = jnp.max(jnp.where(owner_mask[:, :, None, None], page_max[None], -jnp.inf), axis=1)
    slot_max = jnp.maximum(slot_max, own_score)
    weights = jnp.exp(scores - jnp.take(slot_max, page_owner, axis=0)[..., None])
    rounded = weights.astype(jnp.bfloat16)
    page_total = jnp.sum(weights, axis=-1)
    page_numerator = jnp.einsum(
        "pgjt,pgdt->pgjd", rounded, cache_pages[:, 1], preferred_element_type=jnp.float32
    )
    own_weight = jnp.exp(own_score - slot_max)
    own_rounded = lax.optimization_barrier(own_weight.astype(jnp.bfloat16)).astype(jnp.float32)
    owner_float = owner_table.astype(jnp.float32)
    denominator = (
        jnp.einsum("sp,pgj->sgj", owner_float, page_total, precision=lax.Precision.HIGHEST)
        + own_weight
    )
    numerator = jnp.einsum(
        "sp,pgjd->sgjd", owner_float, page_numerator, precision=lax.Precision.HIGHEST
    )
    numerator = numerator + own_rounded[..., None] * own_value.astype(jnp.float32)[:, :, None, :]
    context = (numerator / denominator[..., None]).astype(jnp.bfloat16).reshape(slot_count, -1)
    gathered = lax.all_gather(context, "req", axis=0, tiled=True)
    wanted = first_slot + slot_ids
    selector = (occupant[None, :] == wanted[:, None]).astype(jnp.bfloat16)
    attended = jnp.dot(selector, gathered, preferred_element_type=jnp.float32).astype(jnp.bfloat16)
    partial_value = lax.dot_general(
        attended, w_out, (((1,), (1,)), ((), ())), preferred_element_type=jnp.float32
    )
    summed = lax.psum_scatter(partial_value, "kv", scatter_dimension=1, tiled=True)
    col_share = summed.shape[1]
    residual = lax.dynamic_slice_in_dim(hidden_wide, lax.axis_index("kv") * col_share, col_share, 1)
    return (residual + summed).astype(jnp.bfloat16)


def solution(mesh):
    return jax.shard_map(
        per_device,
        mesh=mesh,
        in_specs=(
            P("req", None),
            P(),
            P(None, "kv"),
            P(None, "kv"),
            P("req", None, "kv", None, None),
            P("req"),
            P("req", None),
            P(),
        ),
        out_specs=P("req", "kv"),
        check_vma=False,
    )
```

profile of v0, /device:TPU:2, one launch (start us, length us, event | category | flops | bytes accessed | tf_op | source)
XLA Modules:
  0.0 147.1 jit_solution(2917014156746804395)
XLA Ops:
  6.5 0.0 copy-start
  6.5 0.0 all-gather.2.cloned.1.call-start
  6.5 1.0 multiply_reduce_fusion
  7.6 1.5 %multiply_convert_fusion = bf16[16,1536]{1,0:T(8,128)(2,1)} fusion(f32[1536]{0:T(1024)} %param.9, f32[16]{0:T(128)S(1)} %add_rsqrt_fusion, bf16[16,1536]{1,0:T(8,128)(2,1)} %param.8), kind=kLoop, calls=%fused_computation.28 | loop fusion | flops 98304 | bytes 104512 | tf_op jit(solution)/shard_map/convert_element_type | solution.py:24
  9.1 0.0 all-gather.2.cloned.1.call-update
  9.1 0.0 reduce-scatter.4.cloned.1.call-start
  9.2 0.8 compare_and_fusion
  10.0 0.7 and_select_fusion
  10.6 0.1 iota_compare_fusion.1
  10.7 1.7 %select_reduce_fusion = (s32[192]{0:T(256)S(1)}, s32[16,192]{1,0:T(8,128)S(1)}) fusion(s32[16,128]{1,0:T(8,128)} %param.14, pred[16,128]{1,0:T(8,128)(4,1)S(1)} %iota_compare_fusion.1), kind=kLoop, calls=%fused_computation.10 | loop fusion | flops 2356032 | bytes 23296 | tf_op jit(solution)/shard_map/reduce_sum | solution.py:43
  12.4 0.7 multiply_reduce_fusion.2
  13.2 0.1 add_compare_fusion
  13.3 47.2 %all-gather.2.cloned.1.call-done = bf16[512,1536]{1,0:T(8,128)(2,1)} async-done(((bf16[16,1536]{1,0:T(8,128)(2,1)}), bf16[512,1536]{1,0:T(8,128)(2,1)}) %all-gather.2.cloned.1.call-update) | async-done | bytes 1572880 | tf_op jit(solution)/shard_map/all_gather | solution.py:26
  60.5 2.2 %gather_fusion = bf16[16,1536]{1,0:T(8,128)(2,1)S(1)} fusion(bf16[512,1536]{1,0:T(8,128)(2,1)} %all-gather.2.cloned.1.call-done, s32[1024]{0:T(1024)S(1)} %pad_clamp_fusion.1), kind=kCustom, calls=%fused_computation | custom fusion | bytes 98368 | tf_op jit(solution)/shard_map/jit(_take)/gather | solution.py:27
  62.7 0.0 copy-done
  62.7 0.3 convolution_convert_fusion
  63.1 0.1 reshape.230
  63.2 0.1 multiply_reduce_fusion.1
  63.3 0.1 copy.28
  63.4 0.8 gather_fusion.1
  64.2 3.8 %fusion.39 = (f32[192,2]{1,0:T(8,128)S(1)}, f32[192,2,128]{2,1,0:T(2,128)S(1)}) fusion(bf16[192,2,1,96,128]{4,3,2,1,0:T(8,128)(2,1)} %param.12, bf16[192,2,96]{2,1,0:T(2,128)(2,1)S(1)} %gather_fusion.1, pred[192]{0:T(512)(128)(4,1)S(1)} %compare_and_fusion.1, pred[192,128]{1,0:T(8,128)(4,1)S(1)} %add_compare_fusion), kind=kOutput, calls=%fused_computation.76 | convolution fusion | flops 9621120 | bytes 5015232 | tf_op jit(solution)/shard_map/pgjd,pgdt->pgjt/dot_general | solution.py:49
  68.1 0.1 copy.27
  68.2 0.1 select_reduce_fusion.1
  68.3 0.1 copy.29
  68.4 0.7 gather_fusion.2
  69.1 0.1 broadcast_select_fusion.2
  69.2 0.0 copy-start.1
  69.2 0.0 copy-start.3
  69.2 5.0 %fusion = f32[192,2,96]{2,1,0:T(2,128)S(1)} fusion(bf16[192,2,1,96,128]{4,3,2,1,0:T(8,128)(2,1)} %param.12, f32[192,2,128]{2,1,0:T(2,128)S(1)} %get-tuple-element.16, f32[192,2]{1,0:T(8,128)S(1)} %broadcast_select_fusion.2), kind=kOutput, calls=%fused_computation.3 | convolution fusion | flops 9535488 | bytes 5064192 | tf_op jit(solution)/shard_map/pgjt,pgdt->pgjd/dot_general | solution.py:66
  74.2 0.5 fusion.16
  74.7 0.0 copy-start.2
  74.8 0.3 convolution_add_fusion.1
  75.0 0.3 fusion.11
  75.3 0.1 reshape.233
  75.4 23.2 %all_gather.7 = bf16[512,192]{1,0:T(8,128)(2,1)S(1)} all-gather(bf16[16,192]{1,0:T(8,128)(2,1)S(1)} %reshape.233), channel_id=1, replica_groups=mesh['req'=32,'kv'=8] {'req'}, dimensions={0}, use_global_device_ids=true | all-gather | bytes 202752 | tf_op jit(solution)/shard_map/all_gather | solution.py:81
  98.6 0.0 copy-done.1
  98.6 0.0 copy-done.3
  98.6 1.5 %convolution_bitcast_fusion = f32[1536,16]{1,0:T(8,128)} fusion(bf16[1536,192]{0,1:T(8,128)(2,1)S(1)} %copy-done.1, bf16[512,192]{1,0:T(8,128)(2,1)S(1)} %all_gather.7, s32[512]{0:T(512)S(1)} %copy-done.3, s32[16]{0:T(128)S(1)} %iota_add_fusion), kind=kOutput, calls=%fused_computation.9 | convolution fusion | flops 12594176 | bytes 886848
  100.1 0.0 reduce-scatter.4.cloned.1.call-update
  100.1 0.0 copy-done.2
  100.2 38.5 %reduce-scatter.4.cloned.1.call-done = f32[192,16]{1,0:T(8,128)} async-done(((f32[1536,16]{1,0:T(8,128)}), f32[192,16]{1,0:T(8,128)}) %reduce-scatter.4.cloned.1.call-update) | async-done | bytes 12304
  138.6 0.9 copy.34
  139.6 0.7 add_convert_fusion
  (14 shorter events, 0.1 us)
Async XLA Ops:
  6.5 56.2 %copy-start = (bf16[1536,384]{1,0:T(8,128)(2,1)S(1)}, bf16[1536,384]{1,0:T(8,128)(2,1)}, u32[]{:S(2)}) copy-start(bf16[1536,384]{1,0:T(8,128)(2,1)} %param.10) | copy-start | bytes 3538948
  6.5 53.9 %all-gather.2.cloned.1.call-start = ((), (), s32[]{:S(2)}) async-start(), calls=%async_computation.1 | async-start | bytes 1622016 | tf_op jit(solution)/shard_map/all_gather | solution.py:26
  9.1 129.5 %reduce-scatter.4.cloned.1.call-start = ((), (), s32[]{:S(2)}) async-start(), calls=%async_computation.2 | async-start | bytes 884736
  69.2 29.5 %copy-start.1 = (bf16[1536,192]{0,1:T(8,128)(2,1)S(1)}, bf16[1536,192]{0,1:T(8,128)(2,1)}, u32[]{:S(2)}) copy-start(bf16[1536,192]{0,1:T(8,128)(2,1)} %param.11) | copy-start | bytes 1769476
  69.2 29.4 %copy-start.3 = (s32[512]{0:T(512)S(1)}, s32[512]{0:T(512)}, u32[]{:S(2)}) copy-start(s32[512]{0:T(512)} %param.15) | copy-start | bytes 6148
  74.7 25.4 %copy-start.2 = (bf16[16,1536]{1,0:T(8,128)(2,1)S(1)}, bf16[16,1536]{1,0:T(8,128)(2,1)}, u32[]{:S(2)}) copy-start(bf16[16,1536]{1,0:T(8,128)(2,1)} %param.8) | copy-start | bytes 147460
Sparse Core Ops, SparseCore 0:
  9.9 50.5 all-gather.1
  100.2 38.3 reduce-scatter.3
where the time goes:
time: 147 us
  waiting for transfers between devices  85.7 us (58%)
  blocking collectives  23.2 us (16%)
  between operations  13.6 us (9%)
  matrix products  11.2 us (8%)
  other arithmetic  8.17 us (6%)
  local copies, waits for them, and re-layouts  5.21 us (4%)
    all_gather x1, waiting for transfers between devices, per_device(): every_normed = lax.all_gather(normed, 'req', axis=0, tiled=True)  47.2 us
    unnamed x3, waiting for transfers between devices  38.5 us
    all_gather x1, blocking collectives, per_device(): gathered = lax.all_gather(context, 'req', axis=0, tiled=True)  23.2 us
    dot_general x1, matrix products, per_device(): jnp.einsum('pgjt,pgdt->pgjd', rounded, cache_pages[:, 1], preferred_eleme...  5.01 us
    dot_general x1, matrix products, per_device(): jnp.einsum('pgjd,pgdt->pgjt', page_queries, cache_pages[:, 0], preferred_...  3.85 us
  transfers between devices with their start and end apart: 2, of which 2 were waited for; matrix products, arithmetic and copies ran while one was open for 3% of the time, Pallas kernels for 0%

commit v1 on v0

--- a/solution.py
+++ b/solution.py
@@ -23,9 +23,9 @@
         * norm_gain
     ).astype(jnp.bfloat16)
     served = lax.dynamic_slice_in_dim(occupant, first_slot, slot_count)
-    every_normed = lax.all_gather(normed, "req", axis=0, tiled=True)
-    picked = jnp.take(every_normed, served, axis=0)
-    slot_rows = jnp.dot(picked, w_qkv, preferred_element_type=jnp.float32).astype(jnp.bfloat16)
+    own_rows = jnp.dot(normed, w_qkv, preferred_element_type=jnp.float32).astype(jnp.bfloat16)
+    every_row = lax.all_gather(own_rows, "req", axis=0, tiled=True)
+    slot_rows = jnp.take(every_row, served, axis=0)
     slot_rows = slot_rows.reshape(slot_count, kv_local, GROUP + 2, HD)
     queries = slot_rows[:, :, :GROUP]
     own_key = slot_rows[:, :, GROUP]

time: 147 us -> 122 us (0.83)
  waiting for transfers between devices: 85.7 us -> 39.9 us
  blocking collectives: 23.2 us -> 47.9 us
  other arithmetic: 8.17 us -> 4.73 us
  local copies, waits for them, and re-layouts: 5.21 us -> 3.54 us
    all_gather x1 -> x0, waiting for transfers between devices: 47.2 us -> none  [per_device(): every_normed = lax.all_gather(normed, 'req', axis=0, tiled=True)]
    all_gather x0 -> x1, blocking collectives: none -> 24.9 us  [per_device(): every_row = lax.all_gather(own_rows, 'req', axis=0, tiled=True)]
    gather x1 -> x2, local copies, waits for them, and re-layouts: 2.25 us -> 0.68 us  [per_device(): slot_rows = jnp.take(every_row, served, axis=0)]
    convert_element_type x1 -> x0, other arithmetic: 1.52 us -> none  [per_device(): normed = (hidden_wide * lax.rsqrt(jnp.mean(hidden_wide * hidden_wide, axi...]
    unnamed x3 -> x2, waiting for transfers between devices: 38.5 us -> 39.9 us
  transfers between devices with their start and end apart: 2 -> 1, of which waited for: 2 -> 1; matrix products, arithmetic and copies ran while one was open for 3% -> 0% of each run, Pallas kernels for 0% -> 0%
where the time goes in v1:
time: 122 us
  blocking collectives  47.9 us (39%)
  waiting for transfers between devices  39.9 us (33%)
  between operations  13.6 us (11%)
  matrix products  12 us (10%)
  other arithmetic  4.73 us (4%)
  local copies, waits for them, and re-layouts  3.54 us (3%)
    unnamed x2, waiting for transfers between devices  39.9 us
    all_gather x1, blocking collectives, per_device(): every_row = lax.all_gather(own_rows, 'req', axis=0, tiled=True)  24.9 us
    all_gather x1, blocking collectives, per_device(): gathered = lax.all_gather(context, 'req', axis=0, tiled=True)  23.1 us
    dot_general x1, matrix products, per_device(): jnp.einsum('pgjt,pgdt->pgjd', rounded, cache_pages[:, 1], preferred_eleme...  5.01 us
    dot_general x1, matrix products, per_device(): jnp.einsum('pgjd,pgdt->pgjt', page_queries, cache_pages[:, 0], preferred_...  3.85 us
  transfers between devices with their start and end apart: 1, of which 1 were waited for; matrix products, arithmetic and copies ran while one was open for 0% of the time, Pallas kernels for 0%

profile of v1, /device:TPU:2, one launch (start us, length us, event | category | flops | bytes accessed | tf_op | source)
XLA Modules:
  0.0 121.8 jit_solution(13815415741669483195)
XLA Ops:
  6.5 0.0 copy-start
  6.5 0.0 copy-start.5
  6.5 0.0 copy-start.3
  6.5 0.0 reduce-scatter.4.cloned.1.call-start
  6.6 0.9 compare_and_fusion
  7.4 0.9 multiply_reduce_fusion
  8.4 0.0 copy-done
  8.4 1.1 convolution_convert_fusion
  9.5 24.9 %all_gather.6 = bf16[512,384]{1,0:T(8,128)(2,1)S(1)} all-gather(bf16[16,384]{1,0:T(8,128)(2,1)S(1)} %convolution_convert_fusion), channel_id=1, replica_groups=mesh['req'=32,'kv'=8] {'req'}, dimensions={0}, use_global_device_ids=true | all-gather | bytes 405504 | tf_op jit(solution)/shard_map/all_gather | solution.py:27
  34.4 0.6 gather_fusion
  35.0 0.1 gather.19
  35.1 0.1 broadcast_select_fusion.3
  35.2 0.0 copy-done.5
  35.2 0.1 iota_compare_fusion.1
  35.3 0.0 copy-done.3
  35.3 1.0 select_reduce_fusion
  36.3 0.1 multiply_reduce_fusion.2
  36.4 0.1 multiply_reduce_fusion.1
  36.5 0.1 copy.29
  36.6 0.8 gather_fusion.1
  37.5 0.1 add_compare_fusion
  37.6 3.8 %fusion.38 = (f32[192,2]{1,0:T(8,128)S(1)}, f32[192,2,128]{2,1,0:T(2,128)S(1)}) fusion(bf16[192,2,1,96,128]{4,3,2,1,0:T(8,128)(2,1)} %param.12, bf16[192,2,96]{2,1,0:T(2,128)(2,1)S(1)} %gather_fusion.1, pred[192]{0:T(512)(128)(4,1)S(1)} %compare_and_fusion.1, pred[192,128]{1,0:T(8,128)(4,1)S(1)} %add_compare_fusion), kind=kOutput, calls=%fused_computation.76 | convolution fusion | flops 9621120 | bytes 5015232 | tf_op jit(solution)/shard_map/pgjd,pgdt->pgjt/dot_general | solution.py:49
  41.4 0.1 copy.28
  41.5 0.1 select_reduce_fusion.1
  41.6 0.1 copy.30
  41.7 0.7 gather_fusion.2
  42.4 0.1 broadcast_select_fusion.2
  42.5 0.5 fusion.16
  43.1 0.0 copy-start.1
  43.1 0.0 copy-start.4
  43.1 5.0 %fusion = f32[192,2,96]{2,1,0:T(2,128)S(1)} fusion(bf16[192,2,1,96,128]{4,3,2,1,0:T(8,128)(2,1)} %param.12, f32[192,2,128]{2,1,0:T(2,128)S(1)} %get-tuple-element.16, f32[192,2]{1,0:T(8,128)S(1)} %broadcast_select_fusion.2), kind=kOutput, calls=%fused_computation.3 | convolution fusion | flops 9535488 | bytes 5064192 | tf_op jit(solution)/shard_map/pgjt,pgdt->pgjd/dot_general | solution.py:66
  48.1 0.0 copy-start.2
  48.1 0.3 convolution_add_fusion.1
  48.4 0.3 fusion.11
  48.7 0.1 reshape.245
  48.7 23.1 %all_gather.7 = bf16[512,192]{1,0:T(8,128)(2,1)S(1)} all-gather(bf16[16,192]{1,0:T(8,128)(2,1)S(1)} %reshape.245), channel_id=1, replica_groups=mesh['req'=32,'kv'=8] {'req'}, dimensions={0}, use_global_device_ids=true | all-gather | bytes 202752 | tf_op jit(solution)/shard_map/all_gather | solution.py:81
  71.8 0.0 copy-done.1
  71.8 0.0 copy-done.4
  71.8 1.5 %convolution_bitcast_fusion = f32[1536,16]{1,0:T(8,128)} fusion(bf16[1536,192]{0,1:T(8,128)(2,1)S(1)} %copy-done.1, bf16[512,192]{1,0:T(8,128)(2,1)S(1)} %all_gather.7, s32[512]{0:T(512)S(1)} %copy-done.4, s32[16]{0:T(128)S(1)} %iota_add_fusion), kind=kOutput, calls=%fused_computation.9 | convolution fusion | flops 12594176 | bytes 886848
  73.3 0.0 reduce-scatter.4.cloned.1.call-update
  73.3 0.0 copy-done.2
  73.3 39.9 %reduce-scatter.4.cloned.1.call-done = f32[192,16]{1,0:T(8,128)} async-done(((f32[1536,16]{1,0:T(8,128)}), f32[192,16]{1,0:T(8,128)}) %reduce-scatter.4.cloned.1.call-update) | async-done | bytes 12304
  113.3 0.9 copy.35
  114.2 0.7 add_convert_fusion
  (15 shorter events, 0.1 us)
Async XLA Ops:
  6.5 1.8 %copy-start = (bf16[1536,384]{1,0:T(8,128)(2,1)S(1)}, bf16[1536,384]{1,0:T(8,128)(2,1)}, u32[]{:S(2)}) copy-start(bf16[1536,384]{1,0:T(8,128)(2,1)} %param.10) | copy-start | bytes 3538948
  6.5 28.7 %copy-start.5 = (s32[16]{0:T(128)S(1)}, s32[16]{0:T(128)}, u32[]{:S(2)}) copy-start(s32[16]{0:T(128)} %param.13) | copy-start | bytes 196
  6.5 28.8 %copy-start.3 = (s32[16,128]{1,0:T(8,128)S(1)}, s32[16,128]{1,0:T(8,128)}, u32[]{:S(2)}) copy-start(s32[16,128]{1,0:T(8,128)} %param.14) | copy-start | bytes 24580
  6.5 106.7 %reduce-scatter.4.cloned.1.call-start = ((), (), s32[]{:S(2)}) async-start(), calls=%async_computation.1 | async-start | bytes 884736
  43.1 28.8 %copy-start.1 = (bf16[1536,192]{0,1:T(8,128)(2,1)S(1)}, bf16[1536,192]{0,1:T(8,128)(2,1)}, u32[]{:S(2)}) copy-start(bf16[1536,192]{0,1:T(8,128)(2,1)} %param.11) | copy-start | bytes 1769476
  43.1 28.7 %copy-start.4 = (s32[512]{0:T(512)S(1)}, s32[512]{0:T(512)}, u32[]{:S(2)}) copy-start(s32[512]{0:T(512)} %param.15) | copy-start | bytes 6148
  48.1 25.2 %copy-start.2 = (bf16[16,1536]{1,0:T(8,128)(2,1)S(1)}, bf16[16,1536]{1,0:T(8,128)(2,1)}, u32[]{:S(2)}) copy-start(bf16[16,1536]{1,0:T(8,128)(2,1)} %param.8) | copy-start | bytes 147460
Sparse Core Ops, SparseCore 0:
  73.4 39.7 reduce-scatter.3

commit v2 on v1

--- a/solution.py
+++ b/solution.py
@@ -9,6 +9,12 @@
 PAGE = 128
 MAXP = 128
 GROUP = 2
+
+
+def exchange(rows, axis):
+    count = lax.axis_size(axis)
+    sent = jnp.broadcast_to(rows[None], (count,) + rows.shape)
+    return lax.all_to_all(sent, axis, 0, 0).reshape(count * rows.shape[0], rows.shape[1])
 
 
 def per_device(hidden, norm_gain, w_qkv, w_out, cache_pages, lengths, page_table, occupant):
@@ -24,7 +30,7 @@
     ).astype(jnp.bfloat16)
     served = lax.dynamic_slice_in_dim(occupant, first_slot, slot_count)
     own_rows = jnp.dot(normed, w_qkv, preferred_element_type=jnp.float32).astype(jnp.bfloat16)
-    every_row = lax.all_gather(own_rows, "req", axis=0, tiled=True)
+    every_row = exchange(own_rows, "req")
     slot_rows = jnp.take(every_row, served, axis=0)
     slot_rows = slot_rows.reshape(slot_count, kv_local, GROUP + 2, HD)
     queries = slot_rows[:, :, :GROUP]
@@ -78,15 +84,17 @@
     )
     numerator = numerator + own_rounded[..., None] * own_value.astype(jnp.float32)[:, :, None, :]
     context = (numerator / denominator[..., None]).astype(jnp.bfloat16).reshape(slot_count, -1)
-    gathered = lax.all_gather(context, "req", axis=0, tiled=True)
+    gathered = exchange(context, "req")
     wanted = first_slot + slot_ids
     selector = (occupant[None, :] == wanted[:, None]).astype(jnp.bfloat16)
     attended = jnp.dot(selector, gathered, preferred_element_type=jnp.float32).astype(jnp.bfloat16)
     partial_value = lax.dot_general(
         attended, w_out, (((1,), (1,)), ((), ())), preferred_element_type=jnp.float32
     )
-    summed = lax.psum_scatter(partial_value, "kv", scatter_dimension=1, tiled=True)
-    col_share = summed.shape[1]
+    kv_count = lax.axis_size("kv")
+    col_share = partial_value.shape[1] // kv_count
+    blocks = partial_value.reshape(slot_count, kv_count, col_share).transpose(1, 0, 2)
+    summed = jnp.sum(lax.all_to_all(blocks, "kv", 0, 0), axis=0)
     residual = lax.dynamic_slice_in_dim(hidden_wide, lax.axis_index("kv") * col_share, col_share, 1)
     return (residual + summed).astype(jnp.bfloat16)
 

time: 122 us -> 67.1 us (0.55)
  the two profiles are of different devices: /device:TPU:2 before, /device:TPU:1 now
where the time goes in v2:
time: 67.1 us; the launch traced here: 66.6 us
  waiting for transfers between devices  25.9 us (39%)
  starting transfers between devices  20.4 us (30%)
  matrix products  10.8 us (16%)
  local copies, waits for them, and re-layouts  5.12 us (8%)
  other arithmetic  4.08 us (6%)
    all_to_all x2, waiting for transfers between devices, exchange(): lax.all_to_all(sent, axis, 0, 0)  17.6 us
    all_to_all x2, starting transfers between devices, exchange(): lax.all_to_all(sent, axis, 0, 0)  12.2 us
    all_to_all x1, waiting for transfers between devices, per_device(): summed = jnp.sum(lax.all_to_all(blocks, 'kv', 0, 0), axis=0)  8.26 us
    all_to_all x1, starting transfers between devices, per_device(): summed = jnp.sum(lax.all_to_all(blocks, 'kv', 0, 0), axis=0)  8.19 us
    dot_general x1, matrix products, per_device(): jnp.einsum('pgjt,pgdt->pgjd', rounded, cache_pages[:, 1], preferred_eleme...  4.95 us
    dot_general x1, matrix products, per_device(): jnp.einsum('pgjd,pgdt->pgjt', page_queries, cache_pages[:, 0], preferred_...  3.85 us
    broadcast_in_dim x3, local copies, waits for them, and re-layouts, exchange(): sent = jnp.broadcast_to(rows[None], (count,) + rows.shape)  1.59 us
  transfers between devices with their start and end apart: 3, of which 3 were waited for; matrix products, arithmetic and copies ran while one was open for 2% of the time, Pallas kernels for 0%

profile of v2, /device:TPU:1, one launch (start us, length us, event | category | flops | bytes accessed | tf_op | source)
XLA Modules:
  0.0 66.6 jit_solution(8634549445276908269)
XLA Ops:
  0.0 0.0 copy-start
  0.0 0.0 copy-start.5
  0.0 0.0 copy-start.3
  0.0 0.0 copy-start.4
  0.0 1.0 %multiply_reduce_fusion = f32[16]{0:T(128)S(1)} fusion(bf16[16,1536]{1,0:T(8,128)(2,1)} %param.8), kind=kLoop, calls=%fused_computation.30 | loop fusion | flops 73712 | bytes 49216 | tf_op jit(solution)/shard_map/reduce_sum | solution.py:28
  1.0 0.2 copy-done
  1.3 1.1 %convolution_convert_fusion = bf16[16,384]{1,0:T(8,128)(2,1)S(1)} fusion(bf16[1536,384]{1,0:T(8,128)(2,1)S(1)} %copy-done, f32[1536]{0:T(1024)} %param.9, f32[16]{0:T(128)S(1)} %add_rsqrt_fusion, bf16[16,1536]{1,0:T(8,128)(2,1)} %param.8), kind=kOutput, calls=%fused_computation.14 | convolution fusion | flops 18978816 | bytes 1247296 | tf_op jit(solution)/shard_map/dot_general | solution.py:32
  2.4 0.8 %broadcast_in_dim.103 = bf16[32,16,384]{2,1,0:T(8,128)(2,1)} broadcast(bf16[16,384]{1,0:T(8,128)(2,1)S(1)} %convolution_convert_fusion), dimensions={1,2} | broadcast | bytes 405504 | tf_op jit(solution)/shard_map/broadcast_in_dim | solution.py:16
  3.2 8.6 %all-to-all-start = ((bf16[32,16,384]{2,1,0:T(8,128)(2,1)}), bf16[32,16,384]{2,1,0:T(8,128)(2,1)S(1)}, u32[]{:S(2)}, u32[]{:S(2)}) async-start(bf16[32,16,384]{2,1,0:T(8,128)(2,1)} %broadcast_in_dim.103), calls=%async_computation | async-start | bytes 786432 | tf_op jit(solution)/shard_map/all_to_all | solution.py:17
  11.8 0.0 copy-done.5
  11.8 0.1 iota_compare_fusion.1
  11.9 0.0 copy-done.3
  11.9 1.0 %select_reduce_fusion = (s32[192]{0:T(256)S(1)}, s32[16,192]{1,0:T(8,128)S(1)}) fusion(s32[16,128]{1,0:T(8,128)S(1)} %copy-done.3, pred[16,128]{1,0:T(8,128)(4,1)S(1)} %iota_compare_fusion.1), kind=kLoop, calls=%fused_computation.9 | loop fusion | flops 2356032 | bytes 23296 | tf_op jit(solution)/shard_map/reduce_sum | solution.py:49
  12.9 0.1 multiply_reduce_fusion.2
  13.0 0.0 copy-done.4
  13.1 0.1 compare_and_fusion
  13.2 0.1 add_compare_fusion
  13.3 8.8 %all-to-all-done = bf16[32,16,384]{2,1,0:T(8,128)(2,1)S(1)} async-done(((bf16[32,16,384]{2,1,0:T(8,128)(2,1)}), bf16[32,16,384]{2,1,0:T(8,128)(2,1)S(1)}, u32[]{:S(2)}, u32[]{:S(2)}) %all-to-all-start) | async-done | bytes 393248 | tf_op jit(solution)/shard_map/all_to_all | solution.py:17
  22.1 0.6 gather_fusion
  22.7 0.1 gather.19
  22.8 0.1 broadcast_select_fusion.3
  22.9 0.1 multiply_reduce_fusion.1
  23.0 0.1 copy.31
  23.1 0.8 %gather_fusion.1 = bf16[192,2,96]{2,1,0:T(2,128)(2,1)S(1)} fusion(bf16[16,2,96]{2,1,0:T(2,128)(2,1)S(1)} %slice_bitcast_fusion, s32[1024]{0:T(1024)S(1)} %pad_clamp_fusion), kind=kCustom, calls=%fused_computation.1 | custom fusion | bytes 148224 | tf_op jit(solution)/shard_map/jit(_take)/gather | solution.py:53
  23.9 3.8 %fusion.39 = (f32[192,2]{1,0:T(8,128)S(1)}, f32[192,2,128]{2,1,0:T(2,128)S(1)}) fusion(bf16[192,2,1,96,128]{4,3,2,1,0:T(8,128)(2,1)} %param.12, bf16[192,2,96]{2,1,0:T(2,128)(2,1)S(1)} %gather_fusion.1, pred[192]{0:T(512)(128)(4,1)S(1)} %compare_and_fusion.1, pred[192,128]{1,0:T(8,128)(4,1)S(1)} %add_compare_fusion), kind=kOutput, calls=%fused_computation.77 | convolution fusion | flops 9621120 | bytes 5015232 | tf_op jit(solution)/shard_map/pgjd,pgdt->pgjt/dot_general | solution.py:55
  27.8 0.1 copy.30
  27.8 0.1 select_reduce_fusion.1
  28.0 0.1 copy.32
  28.0 0.7 %gather_fusion.2 = f32[192,2]{1,0:T(8,128)S(1)} fusion(f32[16,2]{1,0:T(8,128)S(1)} %copy.32, s32[1024]{0:T(1024)S(1)} %pad_clamp_fusion), kind=kCustom, calls=%fused_computation.2 | custom fusion | bytes 3840 | tf_op jit(solution)/shard_map/jit(_take)/gather | solution.py:69
  28.7 0.1 broadcast_select_fusion.2
  28.8 5.0 %fusion = f32[192,2,96]{2,1,0:T(2,128)S(1)} fusion(bf16[192,2,1,96,128]{4,3,2,1,0:T(8,128)(2,1)} %param.12, f32[192,2,128]{2,1,0:T(2,128)S(1)} %get-tuple-element.16, f32[192,2]{1,0:T(8,128)S(1)} %broadcast_select_fusion.2), kind=kOutput, calls=%fused_computation.3 | convolution fusion | flops 9535488 | bytes 5064192 | tf_op jit(solution)/shard_map/pgjt,pgdt->pgjd/dot_general | solution.py:72
  33.8 0.0 copy-start.1
  33.8 0.0 copy-start.2
  33.8 0.5 fusion.17
  34.4 0.3 convolution_add_fusion.1
  34.6 0.3 fusion.11
  34.9 0.1 broadcast_in_dim.113
  35.0 0.7 %broadcast_in_dim.114 = bf16[32,16,192]{2,1,0:T(8,128)(2,1)} broadcast(bf16[16,192]{1,0:T(8,128)(2,1)S(1)} %broadcast_in_dim.113), dimensions={1,2} | broadcast | bytes 202752 | tf_op jit(solution)/shard_map/broadcast_in_dim | solution.py:16
  35.7 3.7 %all-to-all-start.1 = ((bf16[32,16,192]{2,1,0:T(8,128)(2,1)}), bf16[32,16,192]{2,1,0:T(8,128)(2,1)S(1)}, u32[]{:S(2)}, u32[]{:S(2)}) async-start(bf16[32,16,192]{2,1,0:T(8,128)(2,1)} %broadcast_in_dim.114), calls=%async_computation.1 | async-start | bytes 524288 | tf_op jit(solution)/shard_map/all_to_all | solution.py:17
  39.4 8.8 %all-to-all-done.1 = bf16[32,16,192]{2,1,0:T(8,128)(2,1)S(1)} async-done(((bf16[32,16,192]{2,1,0:T(8,128)(2,1)}), bf16[32,16,192]{2,1,0:T(8,128)(2,1)S(1)}, u32[]{:S(2)}, u32[]{:S(2)}) %all-to-all-start.1) | async-done | bytes 196640 | tf_op jit(solution)/shard_map/all_to_all | solution.py:17
  48.2 0.0 copy-done.1
  48.2 0.4 fusion.12
  48.6 0.1 reshape.255
  48.7 0.7 %copy.42 = f32[16,8,192]{2,0,1:T(8,128)} copy(f32[16,8,192]{2,1,0:T(8,128)S(1)} %reshape.255) | data formatting | bytes 196608 | tf_op jit(solution)/shard_map/reshape | solution.py:96
  49.4 8.2 %all-to-all-start.2 = ((f32[8,16,192]{2,1,0:T(8,128)}), f32[8,16,192]{2,1,0:T(8,128)S(1)}, u32[]{:S(2)}, u32[]{:S(2)}) async-start(f32[8,16,192]{2,1,0:T(8,128)} %bitcast.55), calls=%async_computation.2 | async-start | bytes 262144 | tf_op jit(solution)/shard_map/all_to_all | solution.py:97
  57.6 0.0 copy-done.2
  57.6 8.3 %all-to-all-done.2 = f32[8,16,192]{2,1,0:T(8,128)S(1)} async-done(((f32[8,16,192]{2,1,0:T(8,128)}), f32[8,16,192]{2,1,0:T(8,128)S(1)}, u32[]{:S(2)}, u32[]{:S(2)}) %all-to-all-start.2) | async-done | bytes 98336 | tf_op jit(solution)/shard_map/all_to_all | solution.py:97
  65.9 0.7 %add_convert_fusion = bf16[16,192]{1,0:T(8,128)(2,1)} fusion(f32[16,192]{1,0:T(8,128)S(1)} %reduce_sum.82, f32[16,1536]{1,0:T(8,128)S(1)} %convert_element_type.53, s32[]{:T(128)S(6)} %select_n.78), kind=kLoop, calls=%fused_computation.40 | loop fusion | flops 6144 | bytes 30724 | tf_op jit(solution)/shard_map/convert_element_type | solution.py:99
  (16 shorter events, 0.1 us)
Async XLA Ops:
  0.0 1.3 %copy-start = (bf16[1536,384]{1,0:T(8,128)(2,1)S(1)}, bf16[1536,384]{1,0:T(8,128)(2,1)}, u32[]{:S(2)}) copy-start(bf16[1536,384]{1,0:T(8,128)(2,1)} %param.10) | copy-start | bytes 3538948
  0.0 11.8 %copy-start.5 = (s32[16]{0:T(128)S(1)}, s32[16]{0:T(128)}, u32[]{:S(2)}) copy-start(s32[16]{0:T(128)} %param.13) | copy-start | bytes 196
  0.0 11.9 %copy-start.3 = (s32[16,128]{1,0:T(8,128)S(1)}, s32[16,128]{1,0:T(8,128)}, u32[]{:S(2)}) copy-start(s32[16,128]{1,0:T(8,128)} %param.14) | copy-start | bytes 24580
  0.0 13.0 %copy-start.4 = (s32[512]{0:T(512)S(1)}, s32[512]{0:T(512)}, u32[]{:S(2)}) copy-start(s32[512]{0:T(512)} %param.15) | copy-start | bytes 6148
  3.2 18.9 %all-to-all-start = ((bf16[32,16,384]{2,1,0:T(8,128)(2,1)}), bf16[32,16,384]{2,1,0:T(8,128)(2,1)S(1)}, u32[]{:S(2)}, u32[]{:S(2)}) async-start(bf16[32,16,384]{2,1,0:T(8,128)(2,1)} %broadcast_in_dim.103), calls=%async_computation | async-start | bytes 786432 | tf_op jit(solution)/shard_map/all_to_all | solution.py:17
  33.8 14.4 %copy-start.1 = (bf16[1536,192]{0,1:T(8,128)(2,1)S(1)}, bf16[1536,192]{0,1:T(8,128)(2,1)}, u32[]{:S(2)}) copy-start(bf16[1536,192]{0,1:T(8,128)(2,1)} %param.11) | copy-start | bytes 1769476
  33.8 23.8 %copy-start.2 = (bf16[16,1536]{1,0:T(8,128)(2,1)S(1)}, bf16[16,1536]{1,0:T(8,128)(2,1)}, u32[]{:S(2)}) copy-start(bf16[16,1536]{1,0:T(8,128)(2,1)} %param.8) | copy-start | bytes 147460
  35.7 12.5 %all-to-all-start.1 = ((bf16[32,16,192]{2,1,0:T(8,128)(2,1)}), bf16[32,16,192]{2,1,0:T(8,128)(2,1)S(1)}, u32[]{:S(2)}, u32[]{:S(2)}) async-start(bf16[32,16,192]{2,1,0:T(8,128)(2,1)} %broadcast_in_dim.114), calls=%async_computation.1 | async-start | bytes 524288 | tf_op jit(solution)/shard_map/all_to_all | solution.py:17
  49.4 16.5 %all-to-all-start.2 = ((f32[8,16,192]{2,1,0:T(8,128)}), f32[8,16,192]{2,1,0:T(8,128)S(1)}, u32[]{:S(2)}, u32[]{:S(2)}) async-start(f32[8,16,192]{2,1,0:T(8,128)} %bitcast.55), calls=%async_computation.2 | async-start | bytes 262144 | tf_op jit(solution)/shard_map/all_to_all | solution.py:97

commit v3 on v2

--- a/solution.py
+++ b/solution.py
@@ -22,6 +22,7 @@
     pool_size = cache_pages.shape[0]
     kv_local = cache_pages.shape[2]
     first_slot = lax.axis_index("req") * slot_count
+    slot_ids = jnp.arange(slot_count, dtype=jnp.int32)
     hidden_wide = hidden.astype(jnp.float32)
     normed = (
         hidden_wide
@@ -44,43 +45,31 @@
         & live_page[:, :, None]
     ).astype(jnp.int32)
     owner_table = jnp.sum(matches, axis=1)
-    slot_ids = jnp.arange(slot_count, dtype=jnp.int32)
     page_owner = jnp.sum(owner_table * slot_ids[:, None], axis=0)
     page_rank = jnp.sum(matches * jnp.arange(MAXP, dtype=jnp.int32)[None, :, None], axis=(0, 1))
     page_limit = jnp.sum(owner_table * lengths[:, None], axis=0)
     offsets = page_rank[:, None] * PAGE + jnp.arange(PAGE, dtype=jnp.int32)[None, :]
     token_live = offsets < page_limit[:, None]
-    page_queries = jnp.take(queries, page_owner, axis=0)
+    slot_live = (page_owner[None, :, None] == slot_ids[:, None, None]) & token_live[None]
     scores = (
         jnp.einsum(
-            "pgjd,pgdt->pgjt", page_queries, cache_pages[:, 0], preferred_element_type=jnp.float32
+            "sgjd,pgdt->sgjpt", queries, cache_pages[:, 0], preferred_element_type=jnp.float32
         )
         * score_scale
     )
-    scores = jnp.where(token_live[:, None, None, :], scores, -jnp.inf)
-    page_max = jnp.max(scores, axis=-1)
+    scores = jnp.where(slot_live[:, None, None], scores, -jnp.inf)
     own_score = (
         jnp.sum(queries.astype(jnp.float32) * own_key.astype(jnp.float32)[:, :, None, :], axis=-1)
         * score_scale
     )
-    owner_mask = owner_table > 0
-    slot_max = jnp.max(jnp.where(owner_mask[:, :, None, None], page_max[None], -jnp.inf), axis=1)
-    slot_max = jnp.maximum(slot_max, own_score)
-    weights = jnp.exp(scores - jnp.take(slot_max, page_owner, axis=0)[..., None])
+    slot_max = jnp.maximum(jnp.max(scores, axis=(-2, -1)), own_score)
+    weights = jnp.exp(scores - slot_max[..., None, None])
     rounded = weights.astype(jnp.bfloat16)
-    page_total = jnp.sum(weights, axis=-1)
-    page_numerator = jnp.einsum(
-        "pgjt,pgdt->pgjd", rounded, cache_pages[:, 1], preferred_element_type=jnp.float32
-    )
     own_weight = jnp.exp(own_score - slot_max)
     own_rounded = lax.optimization_barrier(own_weight.astype(jnp.bfloat16)).astype(jnp.float32)
-    owner_float = owner_table.astype(jnp.float32)
-    denominator = (
-        jnp.einsum("sp,pgj->sgj", owner_float, page_total, precision=lax.Precision.HIGHEST)
-        + own_weight
-    )
+    denominator = jnp.sum(weights, axis=(-2, -1)) + own_weight
     numerator = jnp.einsum(
-        "sp,pgjd->sgjd", owner_float, page_numerator, precision=lax.Precision.HIGHEST
+        "sgjpt,pgdt->sgjd", rounded, cache_pages[:, 1], preferred_element_type=jnp.float32
     )
     numerator = numerator + own_rounded[..., None] * own_value.astype(jnp.float32)[:, :, None, :]
     context = (numerator / denominator[..., None]).astype(jnp.bfloat16).reshape(slot_count, -1)

time: 67.1 us -> 62.3 us (0.928)
  matrix products: 10.8 us -> 6.83 us
  other arithmetic: 4.08 us -> 7.69 us
  waiting for transfers between devices: 25.9 us -> 22.6 us
  local copies, waits for them, and re-layouts: 5.12 us -> 4.03 us
    dot_general x4 -> x2, matrix products: 9.32 us -> 5.31 us  [the longest x1 3.36 us: per_device(): jnp.einsum('sgjd,pgdt->sgjpt', queries, cache_pages[:, 0], preferred_elem...]
    all_to_all x2, waiting for transfers between devices: 17.6 us -> 14.4 us  [exchange(): lax.all_to_all(sent, axis, 0, 0)]
    gather x2 -> x0, local copies, waits for them, and re-layouts: 1.54 us -> none  [the longest x1 0.83 us: per_device(): page_queries = jnp.take(queries, page_owner, axis=0)]
    unnamed x12 -> x10, local copies, waits for them, and re-layouts: 0.27 us -> 0.96 us
    and x1, other arithmetic: 0.09 us -> 0.77 us  [per_device(): slot_rows = jnp.take(every_row, served, axis=0)]
    reduce_sum x1, other arithmetic: 0.99 us -> 1.66 us  [per_device(): jnp.sum(matches * jnp.arange(MAXP, dtype=jnp.int32)[None, :, None], axis=...]
  transfers between devices with their start and end apart: 3 -> 3, of which waited for: 3 -> 3; matrix products, arithmetic and copies ran while one was open for 2% -> 8% of each run, Pallas kernels for 0% -> 0%
where the time goes in v3:
time: 62.3 us; the launch traced here: 61.7 us
  waiting for transfers between devices  22.6 us (36%)
  starting transfers between devices  20.4 us (33%)
  other arithmetic  7.69 us (12%)
  matrix products  6.83 us (11%)
  local copies, waits for them, and re-layouts  4.03 us (6%)
    all_to_all x2, waiting for transfers between devices, exchange(): lax.all_to_all(sent, axis, 0, 0)  14.4 us
    all_to_all x2, starting transfers between devices, exchange(): lax.all_to_all(sent, axis, 0, 0)  12.2 us
    all_to_all x1, waiting for transfers between devices, per_device(): summed = jnp.sum(lax.all_to_all(blocks, 'kv', 0, 0), axis=0)  8.26 us
    all_to_all x1, starting transfers between devices, per_device(): summed = jnp.sum(lax.all_to_all(blocks, 'kv', 0, 0), axis=0)  8.19 us
    dot_general x1, matrix products, per_device(): jnp.einsum('sgjd,pgdt->sgjpt', queries, cache_pages[:, 0], preferred_elem...  3.36 us
    dot_general x1, matrix products, per_device(): jnp.einsum('sgjpt,pgdt->sgjd', rounded, cache_pages[:, 1], preferred_elem...  1.94 us
    reduce_sum x1, other arithmetic, per_device(): jnp.sum(matches * jnp.arange(MAXP, dtype=jnp.int32)[None, :, None], axis=...  1.66 us
    broadcast_in_dim x3, local copies, waits for them, and re-layouts, exchange(): sent = jnp.broadcast_to(rows[None], (count,) + rows.shape)  1.6 us
  transfers between devices with their start and end apart: 3, of which 3 were waited for; matrix products, arithmetic and copies ran while one was open for 8% of the time, Pallas kernels for 0%

profile of v3, /device:TPU:1, one launch (start us, length us, event | category | flops | bytes accessed | tf_op | source)
XLA Modules:
  0.0 61.7 jit_solution(6995605251451099660)
XLA Ops:
  0.0 0.0 copy-start
  0.0 1.0 %multiply_reduce_fusion = f32[16]{0:T(128)S(1)} fusion(bf16[16,1536]{1,0:T(8,128)(2,1)} %param.8), kind=kLoop, calls=%fused_computation.31 | loop fusion | flops 73712 | bytes 49216 | tf_op jit(solution)/shard_map/reduce_sum | solution.py:29
  1.0 0.3 copy-done
  1.3 1.1 %convolution_convert_fusion = bf16[16,384]{1,0:T(8,128)(2,1)S(1)} fusion(bf16[1536,384]{1,0:T(8,128)(2,1)S(1)} %copy-done, f32[1536]{0:T(1024)} %param.9, f32[16]{0:T(128)S(1)} %add_rsqrt_fusion, bf16[16,1536]{1,0:T(8,128)(2,1)} %param.8), kind=kOutput, calls=%fused_computation.21 | convolution fusion | flops 18978816 | bytes 1247296 | tf_op jit(solution)/shard_map/dot_general | solution.py:33
  2.4 0.8 %broadcast_in_dim.28 = bf16[32,16,384]{2,1,0:T(8,128)(2,1)} broadcast(bf16[16,384]{1,0:T(8,128)(2,1)S(1)} %convolution_convert_fusion), dimensions={1,2} | broadcast | bytes 405504 | tf_op jit(solution)/shard_map/broadcast_in_dim | solution.py:16
  3.2 8.6 %all-to-all-start = ((bf16[32,16,384]{2,1,0:T(8,128)(2,1)}), bf16[32,16,384]{2,1,0:T(8,128)(2,1)S(1)}, u32[]{:S(2)}, u32[]{:S(2)}) async-start(bf16[32,16,384]{2,1,0:T(8,128)(2,1)} %broadcast_in_dim.28), calls=%async_computation | async-start | bytes 786432 | tf_op jit(solution)/shard_map/all_to_all | solution.py:17
  11.8 0.7 %and_select_fusion = s32[16]{0:T(128)S(1)} fusion(s32[16]{0:T(128)} %param.13), kind=kLoop, calls=%fused_computation.55 | loop fusion | flops 256 | bytes 128 | tf_op jit(solution)/shard_map/jit(floor_divide)/jit(_where)/select_n | solution.py:41
  12.5 0.1 iota_compare_fusion.2
  12.5 1.7 %select_reduce_fusion = (s32[192]{0:T(256)S(1)}, s32[16,192]{1,0:T(8,128)S(1)}) fusion(s32[16,128]{1,0:T(8,128)} %param.14, pred[16,128]{1,0:T(8,128)(4,1)S(1)} %iota_compare_fusion.2), kind=kLoop, calls=%fused_computation.16 | loop fusion | flops 2356032 | bytes 23296 | tf_op jit(solution)/shard_map/reduce_sum | solution.py:49
  14.2 0.7 %multiply_reduce_fusion.3 = (s32[192]{0:T(256)S(1)}, s32[192]{0:T(256)S(1)}) fusion(s32[16,192]{1,0:T(8,128)S(1)} %get-tuple-element.8, s32[16]{0:T(128)} %param.13), kind=kLoop, calls=%fused_computation.42 | loop fusion | flops 11904 | bytes 13888 | tf_op jit(solution)/shard_map/reduce_sum | solution.py:48
  15.0 0.1 iota_compare_fusion.1
  15.1 0.1 add_compare_fusion
  15.2 0.8 %compare_and_fusion = (pred[16]{0:T(512)(128)(4,1)S(1)}, s32[16]{0:T(128)S(1)}) fusion(s32[512]{0:T(512)} %param.15, s32[]{:T(128)S(6)} %select_n.32), kind=kLoop, calls=%fused_computation.54 | loop fusion | flops 96 | bytes 148 | tf_op jit(solution)/shard_map/jit(_take)/and | solution.py:35
  16.0 0.6 broadcast_and_fusion
  16.6 5.5 %all-to-all-done = bf16[32,16,384]{2,1,0:T(8,128)(2,1)S(1)} async-done(((bf16[32,16,384]{2,1,0:T(8,128)(2,1)}), bf16[32,16,384]{2,1,0:T(8,128)(2,1)S(1)}, u32[]{:S(2)}, u32[]{:S(2)}) %all-to-all-start) | async-done | bytes 393248 | tf_op jit(solution)/shard_map/all_to_all | solution.py:17
  22.1 0.6 gather_fusion
  22.7 0.1 gather.7
  22.8 0.1 copy_select_fusion
  22.8 0.1 multiply_reduce_fusion.1
  22.9 0.0 copy-start.4
  22.9 3.4 %fusion.8 = (f32[16,2]{0,1:T(2,128)S(1)}, f32[16,2,192,128]{3,0,2,1:T(8,128)S(1)}) fusion(pred[16,192,128]{2,0,1:T(8,128)(4,1)S(1)} %broadcast_and_fusion, bf16[192,2,1,96,128]{4,3,2,1,0:T(8,128)(2,1)} %param.12, bf16[16,1,4,96]{3,0,2,1:T(8,128)(2,1)S(1)} %copy_select_fusion), kind=kOutput, calls=%fused_computation.11 | convolution fusion | flops 153354208 | bytes 8265856 | tf_op jit(solution)/shard_map/sgjd,pgdt->sgjpt/dot_general | solution.py:55
  26.3 1.0 %fusion.6 = f32[16,2]{0,1:T(2,128)S(1)} fusion(f32[16,2,192,128]{3,0,2,1:T(8,128)S(1)} %get-tuple-element.14, f32[16,2]{0,1:T(2,128)S(1)} %multiply_maximum_fusion, pred[16,192,128]{2,0,1:T(8,128)(4,1)S(1)} %broadcast_and_fusion), kind=kLoop, calls=%fused_computation.9 | loop fusion | flops 3145696 | bytes 3539200 | tf_op jit(solution)/shard_map/reduce_sum | solution.py:70
  27.4 0.7 %copy-done.4 = bf16[192,2,1,96,128]{4,3,2,1,0:T(8,128)(2,1)S(1)} copy-done((bf16[192,2,1,96,128]{4,3,2,1,0:T(8,128)(2,1)S(1)}, bf16[192,2,1,96,128]{4,3,2,1,0:T(8,128)(2,1)}, u32[]{:S(2)}) %copy-start.4) | copy-done | bytes 9437208
  28.0 0.0 copy-start.1
  28.1 0.0 copy-start.3
  28.1 0.0 copy-start.2
  28.1 1.9 %fusion.32 = bf16[16,1,2,96]{3,0,2,1:T(8,128)(2,1)S(1)} fusion(bf16[192,2,1,96,128]{4,3,2,1,0:T(8,128)(2,1)S(1)} %copy-done.4, f32[16,2,192,128]{3,0,2,1:T(8,128)S(1)} %get-tuple-element.14, f32[16,2]{0,1:T(2,128)S(1)} %multiply_maximum_fusion, pred[16,192,128]{2,0,1:T(8,128)(4,1)S(1)} %broadcast_and_fusion, f32[16,2]{0,1:T(2,128)S(1)} %exponential_add_fusion, ...), kind=kOutput, calls=%fused_computation.27 | convolution fusion | flops 154152960 | bytes 8274944 | tf_op jit(solution)/shard_map/sgjpt,pgdt->sgjd/dot_general | solution.py:71
  30.0 0.1 broadcast_in_dim.36
  30.1 0.7 %broadcast_in_dim.37 = bf16[32,16,192]{2,1,0:T(8,128)(2,1)} broadcast(bf16[16,192]{1,0:T(8,128)(2,1)S(1)} %broadcast_in_dim.36), dimensions={1,2} | broadcast | bytes 202752 | tf_op jit(solution)/shard_map/broadcast_in_dim | solution.py:16
  30.8 3.7 %all-to-all-start.1 = ((bf16[32,16,192]{2,1,0:T(8,128)(2,1)}), bf16[32,16,192]{2,1,0:T(8,128)(2,1)S(1)}, u32[]{:S(2)}, u32[]{:S(2)}) async-start(bf16[32,16,192]{2,1,0:T(8,128)(2,1)} %broadcast_in_dim.37), calls=%async_computation.1 | async-start | bytes 524288 | tf_op jit(solution)/shard_map/all_to_all | solution.py:17
  34.5 8.8 %all-to-all-done.1 = bf16[32,16,192]{2,1,0:T(8,128)(2,1)S(1)} async-done(((bf16[32,16,192]{2,1,0:T(8,128)(2,1)}), bf16[32,16,192]{2,1,0:T(8,128)(2,1)S(1)}, u32[]{:S(2)}, u32[]{:S(2)}) %all-to-all-start.1) | async-done | bytes 196640 | tf_op jit(solution)/shard_map/all_to_all | solution.py:17
  43.4 0.0 copy-done.1
  43.4 0.0 copy-done.3
  43.4 0.4 fusion.26
  43.8 0.1 reshape.234
  43.9 0.7 %copy.31 = f32[16,8,192]{2,0,1:T(8,128)} copy(f32[16,8,192]{2,1,0:T(8,128)S(1)} %reshape.234) | data formatting | bytes 196608 | tf_op jit(solution)/shard_map/reshape | solution.py:85
  44.5 8.2 %all-to-all-start.2 = ((f32[8,16,192]{2,1,0:T(8,128)}), f32[8,16,192]{2,1,0:T(8,128)S(1)}, u32[]{:S(2)}, u32[]{:S(2)}) async-start(f32[8,16,192]{2,1,0:T(8,128)} %bitcast.107), calls=%async_computation.2 | async-start | bytes 262144 | tf_op jit(solution)/shard_map/all_to_all | solution.py:86
  52.7 0.0 copy-done.2
  52.8 8.3 %all-to-all-done.2 = f32[8,16,192]{2,1,0:T(8,128)S(1)} async-done(((f32[8,16,192]{2,1,0:T(8,128)}), f32[8,16,192]{2,1,0:T(8,128)S(1)}, u32[]{:S(2)}, u32[]{:S(2)}) %all-to-all-start.2) | async-done | bytes 98336 | tf_op jit(solution)/shard_map/all_to_all | solution.py:86
  61.0 0.7 %add_convert_fusion = bf16[16,192]{1,0:T(8,128)(2,1)} fusion(f32[16,192]{1,0:T(8,128)S(1)} %reduce_sum.79, f32[16,1536]{1,0:T(8,128)S(1)} %convert_element_type.48, s32[]{:T(128)S(6)} %select_n.30), kind=kLoop, calls=%fused_computation.39 | loop fusion | flops 6144 | bytes 30724 | tf_op jit(solution)/shard_map/convert_element_type | solution.py:88
  (12 shorter events, 0.1 us)
Async XLA Ops:
  0.0 1.3 %copy-start = (bf16[1536,384]{1,0:T(8,128)(2,1)S(1)}, bf16[1536,384]{1,0:T(8,128)(2,1)}, u32[]{:S(2)}) copy-start(bf16[1536,384]{1,0:T(8,128)(2,1)} %param.10) | copy-start | bytes 3538948
  3.2 18.9 %all-to-all-start = ((bf16[32,16,384]{2,1,0:T(8,128)(2,1)}), bf16[32,16,384]{2,1,0:T(8,128)(2,1)S(1)}, u32[]{:S(2)}, u32[]{:S(2)}) async-start(bf16[32,16,384]{2,1,0:T(8,128)(2,1)} %broadcast_in_dim.28), calls=%async_computation | async-start | bytes 786432 | tf_op jit(solution)/shard_map/all_to_all | solution.py:17
  22.9 5.1 %copy-start.4 = (bf16[192,2,1,96,128]{4,3,2,1,0:T(8,128)(2,1)S(1)}, bf16[192,2,1,96,128]{4,3,2,1,0:T(8,128)(2,1)}, u32[]{:S(2)}) copy-start(bf16[192,2,1,96,128]{4,3,2,1,0:T(8,128)(2,1)} %param.12) | copy-start | bytes 28311556
  28.0 15.3 %copy-start.1 = (bf16[1536,192]{0,1:T(8,128)(2,1)S(1)}, bf16[1536,192]{0,1:T(8,128)(2,1)}, u32[]{:S(2)}) copy-start(bf16[1536,192]{0,1:T(8,128)(2,1)} %param.11) | copy-start | bytes 1769476
  28.1 15.3 %copy-start.3 = (s32[512]{0:T(512)S(1)}, s32[512]{0:T(512)}, u32[]{:S(2)}) copy-start(s32[512]{0:T(512)} %param.15) | copy-start | bytes 6148
  28.1 24.7 %copy-start.2 = (bf16[16,1536]{1,0:T(8,128)(2,1)S(1)}, bf16[16,1536]{1,0:T(8,128)(2,1)}, u32[]{:S(2)}) copy-start(bf16[16,1536]{1,0:T(8,128)(2,1)} %param.8) | copy-start | bytes 147460
  30.8 12.5 %all-to-all-start.1 = ((bf16[32,16,192]{2,1,0:T(8,128)(2,1)}), bf16[32,16,192]{2,1,0:T(8,128)(2,1)S(1)}, u32[]{:S(2)}, u32[]{:S(2)}) async-start(bf16[32,16,192]{2,1,0:T(8,128)(2,1)} %broadcast_in_dim.37), calls=%async_computation.1 | async-start | bytes 524288 | tf_op jit(solution)/shard_map/all_to_all | solution.py:17
  44.5 16.5 %all-to-all-start.2 = ((f32[8,16,192]{2,1,0:T(8,128)}), f32[8,16,192]{2,1,0:T(8,128)S(1)}, u32[]{:S(2)}, u32[]{:S(2)}) async-start(f32[8,16,192]{2,1,0:T(8,128)} %bitcast.107), calls=%async_computation.2 | async-start | bytes 262144 | tf_op jit(solution)/shard_map/all_to_all | solution.py:86

commit v4 on v3

--- a/solution.py
+++ b/solution.py
@@ -64,7 +64,7 @@
     )
     slot_max = jnp.maximum(jnp.max(scores, axis=(-2, -1)), own_score)
     weights = jnp.exp(scores - slot_max[..., None, None])
-    rounded = weights.astype(jnp.bfloat16)
+    rounded = lax.optimization_barrier(weights.astype(jnp.bfloat16))
     own_weight = jnp.exp(own_score - slot_max)
     own_rounded = lax.optimization_barrier(own_weight.astype(jnp.bfloat16)).astype(jnp.float32)
     denominator = jnp.sum(weights, axis=(-2, -1)) + own_weight
@@ -77,12 +77,14 @@
     wanted = first_slot + slot_ids
     selector = (occupant[None, :] == wanted[:, None]).astype(jnp.bfloat16)
     attended = jnp.dot(selector, gathered, preferred_element_type=jnp.float32).astype(jnp.bfloat16)
-    partial_value = lax.dot_general(
-        attended, w_out, (((1,), (1,)), ((), ())), preferred_element_type=jnp.float32
+    kv_count = lax.axis_size("kv")
+    col_share = w_out.shape[0] // kv_count
+    blocks = jnp.einsum(
+        "sa,kca->ksc",
+        attended,
+        w_out.reshape(kv_count, col_share, w_out.shape[1]),
+        preferred_element_type=jnp.float32,
     )
-    kv_count = lax.axis_size("kv")
-    col_share = partial_value.shape[1] // kv_count
-    blocks = partial_value.reshape(slot_count, kv_count, col_share).transpose(1, 0, 2)
     summed = jnp.sum(lax.all_to_all(blocks, "kv", 0, 0), axis=0)
     residual = lax.dynamic_slice_in_dim(hidden_wide, lax.axis_index("kv") * col_share, col_share, 1)
     return (residual + summed).astype(jnp.bfloat16)

time: 62.3 us -> 62.2 us (level)
  matrix products: 6.83 us -> 7.5 us
  local copies, waits for them, and re-layouts: 4.03 us -> 3.4 us
    dot_general x1, matrix products: 0.4 us -> 1.17 us  [per_device(): jnp.einsum('sa,kca->ksc', attended, w_out.reshape(kv_count, col_share, w_...]
where the time goes in v4:
time: 62.2 us; the launch traced here: 61.6 us
  waiting for transfers between devices  22.3 us (36%)
  starting transfers between devices  20.4 us (33%)
  other arithmetic  7.81 us (13%)
  matrix products  7.5 us (12%)
  local copies, waits for them, and re-layouts  3.4 us (5%)
    all_to_all x2, waiting for transfers between devices, exchange(): lax.all_to_all(sent, axis, 0, 0)  14.1 us
    all_to_all x2, starting transfers between devices, exchange(): lax.all_to_all(sent, axis, 0, 0)  12.2 us
    all_to_all x1, waiting for transfers between devices, per_device(): summed = jnp.sum(lax.all_to_all(blocks, 'kv', 0, 0), axis=0)  8.26 us
    all_to_all x1, starting transfers between devices, per_device(): summed = jnp.sum(lax.all_to_all(blocks, 'kv', 0, 0), axis=0)  8.19 us
    dot_general x1, matrix products, per_device(): jnp.einsum('sgjd,pgdt->sgjpt', queries, cache_pages[:, 0], preferred_elem...  3.36 us
    dot_general x1, matrix products, per_device(): jnp.einsum('sgjpt,pgdt->sgjd', rounded, cache_pages[:, 1], preferred_elem...  1.84 us
    reduce_sum x1, other arithmetic, per_device(): jnp.sum(matches * jnp.arange(MAXP, dtype=jnp.int32)[None, :, None], axis=...  1.66 us
    broadcast_in_dim x3, local copies, waits for them, and re-layouts, exchange(): sent = jnp.broadcast_to(rows[None], (count,) + rows.shape)  1.59 us
  transfers between devices with their start and end apart: 3, of which 3 were waited for; matrix products, arithmetic and copies ran while one was open for 8% of the time, Pallas kernels for 0%

profile of v4, /device:TPU:1, one launch (start us, length us, event | category | flops | bytes accessed | tf_op | source)
XLA Modules:
  0.0 61.6 jit_solution(13975356776289440001)
XLA Ops:
  0.0 0.0 copy-start
  0.0 1.0 %multiply_reduce_fusion = f32[16]{0:T(128)S(1)} fusion(bf16[16,1536]{1,0:T(8,128)(2,1)} %param.8), kind=kLoop, calls=%fused_computation.27 | loop fusion | flops 73712 | bytes 49216 | tf_op jit(solution)/shard_map/reduce_sum | solution.py:29
  1.0 0.3 copy-done
  1.3 1.1 %convolution_convert_fusion = bf16[16,384]{1,0:T(8,128)(2,1)S(1)} fusion(bf16[1536,384]{1,0:T(8,128)(2,1)S(1)} %copy-done, f32[1536]{0:T(1024)} %param.9, f32[16]{0:T(128)S(1)} %add_rsqrt_fusion, bf16[16,1536]{1,0:T(8,128)(2,1)} %param.8), kind=kOutput, calls=%fused_computation.18 | convolution fusion | flops 18978816 | bytes 1247296 | tf_op jit(solution)/shard_map/dot_general | solution.py:33
  2.4 0.8 %broadcast_in_dim.28 = bf16[32,16,384]{2,1,0:T(8,128)(2,1)} broadcast(bf16[16,384]{1,0:T(8,128)(2,1)S(1)} %convolution_convert_fusion), dimensions={1,2} | broadcast | bytes 405504 | tf_op jit(solution)/shard_map/broadcast_in_dim | solution.py:16
  3.2 8.6 %all-to-all-start = ((bf16[32,16,384]{2,1,0:T(8,128)(2,1)}), bf16[32,16,384]{2,1,0:T(8,128)(2,1)S(1)}, u32[]{:S(2)}, u32[]{:S(2)}) async-start(bf16[32,16,384]{2,1,0:T(8,128)(2,1)} %broadcast_in_dim.28), calls=%async_computation | async-start | bytes 786432 | tf_op jit(solution)/shard_map/all_to_all | solution.py:17
  11.8 0.7 %and_select_fusion = s32[16]{0:T(128)S(1)} fusion(s32[16]{0:T(128)} %param.13), kind=kLoop, calls=%fused_computation.51 | loop fusion | flops 256 | bytes 128 | tf_op jit(solution)/shard_map/jit(floor_divide)/jit(_where)/select_n | solution.py:41
  12.5 0.1 iota_compare_fusion.2
  12.5 1.7 %select_reduce_fusion = (s32[192]{0:T(256)S(1)}, s32[16,192]{1,0:T(8,128)S(1)}) fusion(s32[16,128]{1,0:T(8,128)} %param.14, pred[16,128]{1,0:T(8,128)(4,1)S(1)} %iota_compare_fusion.2), kind=kLoop, calls=%fused_computation.13 | loop fusion | flops 2356032 | bytes 23296 | tf_op jit(solution)/shard_map/reduce_sum | solution.py:49
  14.2 0.7 %multiply_reduce_fusion.3 = (s32[192]{0:T(256)S(1)}, s32[192]{0:T(256)S(1)}) fusion(s32[16,192]{1,0:T(8,128)S(1)} %get-tuple-element.8, s32[16]{0:T(128)} %param.13), kind=kLoop, calls=%fused_computation.38 | loop fusion | flops 11904 | bytes 13888 | tf_op jit(solution)/shard_map/reduce_sum | solution.py:48
  15.0 0.1 iota_compare_fusion.1
  15.1 0.1 add_compare_fusion
  15.2 0.8 %compare_and_fusion = (pred[16]{0:T(512)(128)(4,1)S(1)}, s32[16]{0:T(128)S(1)}) fusion(s32[512]{0:T(512)} %param.15, s32[]{:T(128)S(6)} %select_n.32), kind=kLoop, calls=%fused_computation.50 | loop fusion | flops 96 | bytes 148 | tf_op jit(solution)/shard_map/jit(_take)/and | solution.py:35
  16.0 0.6 broadcast_and_fusion
  16.6 5.5 %all-to-all-done = bf16[32,16,384]{2,1,0:T(8,128)(2,1)S(1)} async-done(((bf16[32,16,384]{2,1,0:T(8,128)(2,1)}), bf16[32,16,384]{2,1,0:T(8,128)(2,1)S(1)}, u32[]{:S(2)}, u32[]{:S(2)}) %all-to-all-start) | async-done | bytes 393248 | tf_op jit(solution)/shard_map/all_to_all | solution.py:17
  22.1 0.6 gather_fusion
  22.7 0.1 gather.7
  22.8 0.1 copy_select_fusion
  22.8 0.1 multiply_reduce_fusion.1
  22.9 0.0 copy-start.4
  22.9 3.4 %fusion.8 = (f32[16,2]{0,1:T(2,128)S(1)}, f32[16,2,192,128]{3,0,2,1:T(8,128)S(1)}) fusion(pred[16,192,128]{2,0,1:T(8,128)(4,1)S(1)} %broadcast_and_fusion, bf16[192,2,1,96,128]{4,3,2,1,0:T(8,128)(2,1)} %param.12, bf16[16,1,4,96]{3,0,2,1:T(8,128)(2,1)S(1)} %copy_select_fusion), kind=kOutput, calls=%fused_computation.11 | convolution fusion | flops 153354208 | bytes 8265856 | tf_op jit(solution)/shard_map/sgjd,pgdt->sgjpt/dot_general | solution.py:55
  26.3 1.1 %fusion.6 = (f32[16,2]{0,1:T(2,128)S(1)}, bf16[16,1,2,192,128]{4,0,3,2,1:T(8,128)(2,1)S(1)}) fusion(f32[16,2,192,128]{3,0,2,1:T(8,128)S(1)} %get-tuple-element.16, f32[16,2]{0,1:T(2,128)S(1)} %multiply_maximum_fusion, pred[16,192,128]{2,0,1:T(8,128)(4,1)S(1)} %broadcast_and_fusion), kind=kLoop, calls=%fused_computation.9 | loop fusion | flops 3932128 | bytes 5112064 | tf_op jit(solution)/shard_map/reduce_sum | solution.py:70
  27.5 0.6 copy-done.4
  28.0 0.0 copy-start.1
  28.1 0.0 copy-start.3
  28.1 1.8 %fusion.27 = bf16[16,1,2,96]{3,0,2,1:T(8,128)(2,1)S(1)} fusion(bf16[192,2,1,96,128]{4,3,2,1,0:T(8,128)(2,1)S(1)} %copy-done.4, bf16[16,1,2,192,128]{4,0,3,2,1:T(8,128)(2,1)S(1)} %get-tuple-element.12, f32[16,2]{0,1:T(2,128)S(1)} %exponential_add_fusion, f32[16,96]{1,0:T(8,128)S(1)} %get-tuple-element.13, f32[16,2]{0,1:T(2,128)S(1)} %bitcast_convert_fusion), kind=kOutput, calls=%fused_computation.24 | convolution fusion | flops 151007232 | bytes 6307840 | tf_op jit(solution)/shard_map/sgjpt,pgdt->sgjd/dot_general | solution.py:71
  29.9 0.0 copy-start.2
  29.9 0.1 broadcast_in_dim.36
  30.0 0.7 %broadcast_in_dim.37 = bf16[32,16,192]{2,1,0:T(8,128)(2,1)} broadcast(bf16[16,192]{1,0:T(8,128)(2,1)S(1)} %broadcast_in_dim.36), dimensions={1,2} | broadcast | bytes 202752 | tf_op jit(solution)/shard_map/broadcast_in_dim | solution.py:16
  30.7 3.7 %all-to-all-start.1 = ((bf16[32,16,192]{2,1,0:T(8,128)(2,1)}), bf16[32,16,192]{2,1,0:T(8,128)(2,1)S(1)}, u32[]{:S(2)}, u32[]{:S(2)}) async-start(bf16[32,16,192]{2,1,0:T(8,128)(2,1)} %broadcast_in_dim.37), calls=%async_computation.1 | async-start | bytes 524288 | tf_op jit(solution)/shard_map/all_to_all | solution.py:17
  34.4 0.0 copy-done.1
  34.4 0.3 copy.24
  34.7 8.6 %all-to-all-done.1 = bf16[32,16,192]{2,1,0:T(8,128)(2,1)S(1)} async-done(((bf16[32,16,192]{2,1,0:T(8,128)(2,1)}), bf16[32,16,192]{2,1,0:T(8,128)(2,1)S(1)}, u32[]{:S(2)}, u32[]{:S(2)}) %all-to-all-start.1) | async-done | bytes 196640 | tf_op jit(solution)/shard_map/all_to_all | solution.py:17
  43.3 0.0 copy-done.3
  43.3 1.2 %convolution_bitcast_fusion = f32[8,16,192]{2,1,0:T(8,128)} fusion(bf16[8,192,192]{2,1,0:T(8,128)(2,1)S(1)} %bitcast.101, bf16[512,192]{1,0:T(8,128)(2,1)S(1)} %bitcast.102, s32[512]{0:T(512)S(1)} %copy-done.3, s32[16]{0:T(128)S(1)} %iota_add_fusion), kind=kOutput, calls=%fused_computation.17 | convolution fusion | flops 12594176 | bytes 886848 | tf_op jit(solution)/shard_map/sa,kca->ksc/dot_general | solution.py:82
  44.4 8.2 %all-to-all-start.2 = ((f32[8,16,192]{2,1,0:T(8,128)}), f32[8,16,192]{2,1,0:T(8,128)S(1)}, u32[]{:S(2)}, u32[]{:S(2)}) async-start(f32[8,16,192]{2,1,0:T(8,128)} %convolution_bitcast_fusion), calls=%async_computation.2 | async-start | bytes 262144 | tf_op jit(solution)/shard_map/all_to_all | solution.py:88
  52.6 0.0 copy-done.2
  52.6 8.3 %all-to-all-done.2 = f32[8,16,192]{2,1,0:T(8,128)S(1)} async-done(((f32[8,16,192]{2,1,0:T(8,128)}), f32[8,16,192]{2,1,0:T(8,128)S(1)}, u32[]{:S(2)}, u32[]{:S(2)}) %all-to-all-start.2) | async-done | bytes 98336 | tf_op jit(solution)/shard_map/all_to_all | solution.py:88
  60.9 0.7 %add_convert_fusion = bf16[16,192]{1,0:T(8,128)(2,1)} fusion(f32[16,192]{1,0:T(8,128)S(1)} %reduce_sum.79, f32[16,1536]{1,0:T(8,128)S(1)} %convert_element_type.48, s32[]{:T(128)S(6)} %select_n.30), kind=kLoop, calls=%fused_computation.35 | loop fusion | flops 6144 | bytes 30724 | tf_op jit(solution)/shard_map/convert_element_type | solution.py:90
  (12 shorter events, 0.1 us)
Async XLA Ops:
  0.0 1.3 %copy-start = (bf16[1536,384]{1,0:T(8,128)(2,1)S(1)}, bf16[1536,384]{1,0:T(8,128)(2,1)}, u32[]{:S(2)}) copy-start(bf16[1536,384]{1,0:T(8,128)(2,1)} %param.10) | copy-start | bytes 3538948
  3.2 18.9 %all-to-all-start = ((bf16[32,16,384]{2,1,0:T(8,128)(2,1)}), bf16[32,16,384]{2,1,0:T(8,128)(2,1)S(1)}, u32[]{:S(2)}, u32[]{:S(2)}) async-start(bf16[32,16,384]{2,1,0:T(8,128)(2,1)} %broadcast_in_dim.28), calls=%async_computation | async-start | bytes 786432 | tf_op jit(solution)/shard_map/all_to_all | solution.py:17
  22.9 5.1 %copy-start.4 = (bf16[192,2,1,96,128]{4,3,2,1,0:T(8,128)(2,1)S(1)}, bf16[192,2,1,96,128]{4,3,2,1,0:T(8,128)(2,1)}, u32[]{:S(2)}) copy-start(bf16[192,2,1,96,128]{4,3,2,1,0:T(8,128)(2,1)} %param.12) | copy-start | bytes 28311556
  28.0 6.3 %copy-start.1 = (bf16[1536,192]{0,1:T(8,128)(2,1)S(1)}, bf16[1536,192]{0,1:T(8,128)(2,1)}, u32[]{:S(2)}) copy-start(bf16[1536,192]{0,1:T(8,128)(2,1)} %param.11) | copy-start | bytes 1769476
  28.1 15.2 %copy-start.3 = (s32[512]{0:T(512)S(1)}, s32[512]{0:T(512)}, u32[]{:S(2)}) copy-start(s32[512]{0:T(512)} %param.15) | copy-start | bytes 6148
  29.9 22.7 %copy-start.2 = (bf16[16,1536]{1,0:T(8,128)(2,1)S(1)}, bf16[16,1536]{1,0:T(8,128)(2,1)}, u32[]{:S(2)}) copy-start(bf16[16,1536]{1,0:T(8,128)(2,1)} %param.8) | copy-start | bytes 147460
  30.7 12.5 %all-to-all-start.1 = ((bf16[32,16,192]{2,1,0:T(8,128)(2,1)}), bf16[32,16,192]{2,1,0:T(8,128)(2,1)S(1)}, u32[]{:S(2)}, u32[]{:S(2)}) async-start(bf16[32,16,192]{2,1,0:T(8,128)(2,1)} %broadcast_in_dim.37), calls=%async_computation.1 | async-start | bytes 524288 | tf_op jit(solution)/shard_map/all_to_all | solution.py:17
  44.4 16.5 %all-to-all-start.2 = ((f32[8,16,192]{2,1,0:T(8,128)}), f32[8,16,192]{2,1,0:T(8,128)S(1)}, u32[]{:S(2)}, u32[]{:S(2)}) async-start(f32[8,16,192]{2,1,0:T(8,128)} %convolution_bitcast_fusion), calls=%async_computation.2 | async-start | bytes 262144 | tf_op jit(solution)/shard_map/all_to_all | solution.py:88

commit v5 on v4

--- a/solution.py
+++ b/solution.py
@@ -73,19 +73,19 @@
     )
     numerator = numerator + own_rounded[..., None] * own_value.astype(jnp.float32)[:, :, None, :]
     context = (numerator / denominator[..., None]).astype(jnp.bfloat16).reshape(slot_count, -1)
-    gathered = exchange(context, "req")
-    wanted = first_slot + slot_ids
-    selector = (occupant[None, :] == wanted[:, None]).astype(jnp.bfloat16)
-    attended = jnp.dot(selector, gathered, preferred_element_type=jnp.float32).astype(jnp.bfloat16)
     kv_count = lax.axis_size("kv")
     col_share = w_out.shape[0] // kv_count
     blocks = jnp.einsum(
         "sa,kca->ksc",
-        attended,
+        context,
         w_out.reshape(kv_count, col_share, w_out.shape[1]),
         preferred_element_type=jnp.float32,
     )
-    summed = jnp.sum(lax.all_to_all(blocks, "kv", 0, 0), axis=0)
+    slot_sums = jnp.sum(lax.all_to_all(blocks, "kv", 0, 0), axis=0)
+    every_sum = exchange(slot_sums, "req")
+    inverse = jnp.zeros_like(occupant).at[occupant].set(jnp.arange(occupant.shape[0], dtype=jnp.int32))
+    wanted = lax.dynamic_slice_in_dim(inverse, first_slot, slot_count)
+    summed = jnp.take(every_sum, wanted, axis=0)
     residual = lax.dynamic_slice_in_dim(hidden_wide, lax.axis_index("kv") * col_share, col_share, 1)
     return (residual + summed).astype(jnp.bfloat16)
 

time: 62.2 us -> 67.2 us (1.080)
  local copies, waits for them, and re-layouts: 3.4 us -> 7.63 us
  starting transfers between devices: 20.4 us -> 21.8 us
    scatter x0 -> x1, local copies, waits for them, and re-layouts: none -> 2.44 us  [per_device(): jnp.zeros_like(occupant).at[occupant]]
    all_to_all x2, starting transfers between devices: 12.2 us -> 13.6 us  [exchange(): lax.all_to_all(sent, axis, 0, 0)]
    reshape x1, local copies, waits for them, and re-layouts: 0.27 us -> 1.33 us  [per_device(): w_out.reshape(kv_count, col_share, w_out.shape[1])]
    all_to_all x2, waiting for transfers between devices: 14.1 us -> 13.3 us  [exchange(): lax.all_to_all(sent, axis, 0, 0)]
    broadcast_in_dim x3 -> x2, local copies, waits for them, and re-layouts: 1.59 us -> 1.64 us  [exchange(): sent = jnp.broadcast_to(rows[None], (count,) + rows.shape)]
  transfers between devices with their start and end apart: 3 -> 3, of which waited for: 3 -> 3; matrix products, arithmetic and copies ran while one was open for 8% -> 13% of each run, Pallas kernels for 0% -> 0%
where the time goes in v5:
time: 67.2 us; the launch traced here: 66.6 us
  starting transfers between devices  21.8 us (32%)
  waiting for transfers between devices  21.8 us (32%)
  other arithmetic  7.87 us (12%)
  local copies, waits for them, and re-layouts  7.63 us (11%)
  matrix products  7.29 us (11%)
    all_to_all x2, starting transfers between devices, exchange(): lax.all_to_all(sent, axis, 0, 0)  13.6 us
    all_to_all x2, waiting for transfers between devices, exchange(): lax.all_to_all(sent, axis, 0, 0)  13.3 us
    all_to_all x1, waiting for transfers between devices, per_device(): slot_sums = jnp.sum(lax.all_to_all(blocks, 'kv', 0, 0), axis=0)  8.53 us
    all_to_all x1, starting transfers between devices, per_device(): slot_sums = jnp.sum(lax.all_to_all(blocks, 'kv', 0, 0), axis=0)  8.19 us
    dot_general x1, matrix products, per_device(): jnp.einsum('sgjd,pgdt->sgjpt', queries, cache_pages[:, 0], preferred_elem...  3.36 us
    scatter x1, local copies, waits for them, and re-layouts, per_device(): jnp.zeros_like(occupant).at[occupant]  2.44 us
    dot_general x1, matrix products, per_device(): jnp.einsum('sgjpt,pgdt->sgjd', rounded, cache_pages[:, 1], preferred_elem...  1.84 us
    reduce_sum x1, other arithmetic, per_device(): jnp.sum(matches * jnp.arange(MAXP, dtype=jnp.int32)[None, :, None], axis=...  1.66 us
  transfers between devices with their start and end apart: 3, of which 3 were waited for; matrix products, arithmetic and copies ran while one was open for 13% of the time, Pallas kernels for 0%

profile of v5, /device:TPU:1, one launch (start us, length us, event | category | flops | bytes accessed | tf_op | source)
XLA Modules:
  0.0 66.6 jit_solution(6603781248387443687)
XLA Ops:
  0.0 0.0 copy-start
  0.0 1.0 %multiply_reduce_fusion = f32[16]{0:T(128)S(1)} fusion(bf16[16,1536]{1,0:T(8,128)(2,1)} %param.8), kind=kLoop, calls=%fused_computation.27 | loop fusion | flops 73712 | bytes 49216 | tf_op jit(solution)/shard_map/reduce_sum | solution.py:29
  1.0 0.3 copy-done
  1.3 1.1 %convolution_convert_fusion = bf16[16,384]{1,0:T(8,128)(2,1)S(1)} fusion(bf16[1536,384]{1,0:T(8,128)(2,1)S(1)} %copy-done, f32[1536]{0:T(1024)} %param.9, f32[16]{0:T(128)S(1)} %add_rsqrt_fusion, bf16[16,1536]{1,0:T(8,128)(2,1)} %param.8), kind=kOutput, calls=%fused_computation.20 | convolution fusion | flops 18978816 | bytes 1247296 | tf_op jit(solution)/shard_map/dot_general | solution.py:33
  2.4 0.8 %broadcast_in_dim.43 = bf16[32,16,384]{2,1,0:T(8,128)(2,1)} broadcast(bf16[16,384]{1,0:T(8,128)(2,1)S(1)} %convolution_convert_fusion), dimensions={1,2} | broadcast | bytes 405504 | tf_op jit(solution)/shard_map/broadcast_in_dim | solution.py:16
  3.2 8.6 %all-to-all-start = ((bf16[32,16,384]{2,1,0:T(8,128)(2,1)}), bf16[32,16,384]{2,1,0:T(8,128)(2,1)S(1)}, u32[]{:S(2)}, u32[]{:S(2)}) async-start(bf16[32,16,384]{2,1,0:T(8,128)(2,1)} %broadcast_in_dim.43), calls=%async_computation | async-start | bytes 786432 | tf_op jit(solution)/shard_map/all_to_all | solution.py:17
  11.8 0.7 %and_select_fusion = s32[16]{0:T(128)S(1)} fusion(s32[16]{0:T(128)} %param.13), kind=kLoop, calls=%fused_computation.51 | loop fusion | flops 256 | bytes 128 | tf_op jit(solution)/shard_map/jit(floor_divide)/jit(_where)/select_n | solution.py:41
  12.5 0.1 iota_compare_fusion.2
  12.5 1.7 %select_reduce_fusion = (s32[192]{0:T(256)S(1)}, s32[16,192]{1,0:T(8,128)S(1)}) fusion(s32[16,128]{1,0:T(8,128)} %param.14, pred[16,128]{1,0:T(8,128)(4,1)S(1)} %iota_compare_fusion.2), kind=kLoop, calls=%fused_computation.15 | loop fusion | flops 2356032 | bytes 23296 | tf_op jit(solution)/shard_map/reduce_sum | solution.py:49
  14.2 0.7 %multiply_reduce_fusion.3 = (s32[192]{0:T(256)S(1)}, s32[192]{0:T(256)S(1)}) fusion(s32[16,192]{1,0:T(8,128)S(1)} %get-tuple-element.8, s32[16]{0:T(128)} %param.13), kind=kLoop, calls=%fused_computation.37 | loop fusion | flops 11904 | bytes 13888 | tf_op jit(solution)/shard_map/reduce_sum | solution.py:48
  15.0 0.1 iota_compare_fusion.1
  15.1 0.1 add_compare_fusion
  15.2 0.8 %compare_and_fusion = (pred[16]{0:T(512)(128)(4,1)S(1)}, s32[16]{0:T(128)S(1)}) fusion(s32[512]{0:T(512)} %param.15, s32[]{:T(128)S(6)} %select_n.44), kind=kLoop, calls=%fused_computation.50 | loop fusion | flops 96 | bytes 148 | tf_op jit(solution)/shard_map/jit(_take)/and | solution.py:35
  16.0 1.3 %copy.24 = bf16[1536,192]{1,0:T(8,128)(2,1)S(1)} copy(bf16[1536,192]{0,1:T(8,128)(2,1)} %param.11) | data formatting | bytes 1179648 | tf_op jit(solution)/shard_map/reshape | solution.py:81
  17.3 0.6 broadcast_and_fusion
  17.9 4.2 %all-to-all-done = bf16[32,16,384]{2,1,0:T(8,128)(2,1)S(1)} async-done(((bf16[32,16,384]{2,1,0:T(8,128)(2,1)}), bf16[32,16,384]{2,1,0:T(8,128)(2,1)S(1)}, u32[]{:S(2)}, u32[]{:S(2)}) %all-to-all-start) | async-done | bytes 393248 | tf_op jit(solution)/shard_map/all_to_all | solution.py:17
  22.1 0.6 gather_fusion
  22.7 0.1 gather.11
  22.8 0.1 copy_select_fusion
  22.8 0.1 multiply_reduce_fusion.1
  22.9 0.0 copy-start.3
  22.9 3.4 %fusion.8 = (f32[16,2]{0,1:T(2,128)S(1)}, f32[16,2,192,128]{3,0,2,1:T(8,128)S(1)}) fusion(pred[16,192,128]{2,0,1:T(8,128)(4,1)S(1)} %broadcast_and_fusion, bf16[192,2,1,96,128]{4,3,2,1,0:T(8,128)(2,1)} %param.12, bf16[16,1,4,96]{3,0,2,1:T(8,128)(2,1)S(1)} %copy_select_fusion), kind=kOutput, calls=%fused_computation.13 | convolution fusion | flops 153354208 | bytes 8265856 | tf_op jit(solution)/shard_map/sgjd,pgdt->sgjpt/dot_general | solution.py:55
  26.3 1.1 %fusion.6 = (f32[16,2]{0,1:T(2,128)S(1)}, bf16[16,1,2,192,128]{4,0,3,2,1:T(8,128)(2,1)S(1)}) fusion(f32[16,2,192,128]{3,0,2,1:T(8,128)S(1)} %get-tuple-element.18, f32[16,2]{0,1:T(2,128)S(1)} %multiply_maximum_fusion, pred[16,192,128]{2,0,1:T(8,128)(4,1)S(1)} %broadcast_and_fusion), kind=kLoop, calls=%fused_computation.11 | loop fusion | flops 3932128 | bytes 5112064 | tf_op jit(solution)/shard_map/reduce_sum | solution.py:70
  27.5 0.6 copy-done.3
  28.0 0.0 copy-start.1
  28.1 0.0 copy-start.2
  28.1 1.8 %fusion.26 = bf16[16,1,2,96]{3,0,2,1:T(8,128)(2,1)S(1)} fusion(bf16[192,2,1,96,128]{4,3,2,1,0:T(8,128)(2,1)S(1)} %copy-done.3, bf16[16,1,2,192,128]{4,0,3,2,1:T(8,128)(2,1)S(1)} %get-tuple-element.14, f32[16,2]{0,1:T(2,128)S(1)} %exponential_add_fusion, f32[16,96]{1,0:T(8,128)S(1)} %get-tuple-element.15, f32[16,2]{0,1:T(2,128)S(1)} %bitcast_convert_fusion), kind=kOutput, calls=%fused_computation.24 | convolution fusion | flops 151007232 | bytes 6307840 | tf_op jit(solution)/shard_map/sgjpt,pgdt->sgjd/dot_general | solution.py:71
  29.9 0.1 reshape.273
  30.0 1.0 %convolution_bitcast_fusion = f32[8,16,192]{2,1,0:T(8,128)} fusion(bf16[16,192,1]{1,0,2:T(8,128)(2,1)S(1)} %reshape.273, bf16[8,192,192]{2,1,0:T(8,128)(2,1)S(1)} %bitcast.97), kind=kOutput, calls=%fused_computation.19 | convolution fusion | flops 9437184 | bytes 694272 | tf_op jit(solution)/shard_map/sa,kca->ksc/dot_general | solution.py:78
  31.0 8.2 %all-to-all-start.1 = ((f32[8,16,192]{2,1,0:T(8,128)}), f32[8,16,192]{2,1,0:T(8,128)S(1)}, u32[]{:S(2)}, u32[]{:S(2)}) async-start(f32[8,16,192]{2,1,0:T(8,128)} %convolution_bitcast_fusion), calls=%async_computation.1 | async-start | bytes 262144 | tf_op jit(solution)/shard_map/all_to_all | solution.py:84
  39.2 0.0 copy-done.1
  39.2 8.5 %all-to-all-done.1 = f32[8,16,192]{2,1,0:T(8,128)S(1)} async-done(((f32[8,16,192]{2,1,0:T(8,128)}), f32[8,16,192]{2,1,0:T(8,128)S(1)}, u32[]{:S(2)}, u32[]{:S(2)}) %all-to-all-start.1) | async-done | bytes 98336 | tf_op jit(solution)/shard_map/all_to_all | solution.py:84
  47.7 0.8 %broadcast_in_dim.47 = f32[32,16,192]{2,1,0:T(8,128)} broadcast(f32[16,192]{1,0:T(8,128)S(1)} %reduce_sum.79), dimensions={1,2} | broadcast | bytes 405504 | tf_op jit(solution)/shard_map/broadcast_in_dim | solution.py:16
  48.6 5.0 %all-to-all-start.2 = ((f32[32,16,192]{2,1,0:T(8,128)}), f32[32,16,192]{2,1,0:T(8,128)S(1)}, u32[]{:S(2)}, u32[]{:S(2)}) async-start(f32[32,16,192]{2,1,0:T(8,128)} %broadcast_in_dim.47), calls=%async_computation.2 | async-start | bytes 1048576 | tf_op jit(solution)/shard_map/all_to_all | solution.py:17
  53.6 0.0 copy-done.2
  53.6 2.4 %scatter_custom_fusion = s32[512]{0:T(512)S(1)} fusion(s32[512]{0:T(512)S(1)} %compare_select_fusion, s32[512]{0:T(512)S(1)} %iota.36, s32[]{:T(128)} %constant.33.clone.1), kind=kCustom, calls=%fused_computation.60 | custom fusion | bytes 2052 | tf_op jit(solution)/shard_map/scatter | solution.py:86
  56.1 0.1 compare_and_fusion.1
  56.2 9.1 %all-to-all-done.2 = f32[32,16,192]{2,1,0:T(8,128)S(1)} async-done(((f32[32,16,192]{2,1,0:T(8,128)}), f32[32,16,192]{2,1,0:T(8,128)S(1)}, u32[]{:S(2)}, u32[]{:S(2)}) %all-to-all-start.2) | async-done | bytes 393248 | tf_op jit(solution)/shard_map/all_to_all | solution.py:17
  65.3 0.6 gather_fusion.1
  65.9 0.7 %add_convert_fusion = bf16[16,192]{1,0:T(8,128)(2,1)} fusion(f32[16,192]{1,0:T(8,128)S(1)} %gather_fusion.1, f32[16,1536]{1,0:T(8,128)S(1)} %convert_element_type.44, s32[]{:T(128)S(6)} %select_n.42, pred[16]{0:T(512)(128)(4,1)S(1)} %get-tuple-element.9), kind=kLoop, calls=%fused_computation.34 | loop fusion | flops 9216 | bytes 30740 | tf_op jit(solution)/shard_map/convert_element_type | solution.py:90
  (14 shorter events, 0.1 us)
Async XLA Ops:
  0.0 1.3 %copy-start = (bf16[1536,384]{1,0:T(8,128)(2,1)S(1)}, bf16[1536,384]{1,0:T(8,128)(2,1)}, u32[]{:S(2)}) copy-start(bf16[1536,384]{1,0:T(8,128)(2,1)} %param.10) | copy-start | bytes 3538948
  3.2 18.9 %all-to-all-start = ((bf16[32,16,384]{2,1,0:T(8,128)(2,1)}), bf16[32,16,384]{2,1,0:T(8,128)(2,1)S(1)}, u32[]{:S(2)}, u32[]{:S(2)}) async-start(bf16[32,16,384]{2,1,0:T(8,128)(2,1)} %broadcast_in_dim.43), calls=%async_computation | async-start | bytes 786432 | tf_op jit(solution)/shard_map/all_to_all | solution.py:17
  22.9 5.1 %copy-start.3 = (bf16[192,2,1,96,128]{4,3,2,1,0:T(8,128)(2,1)S(1)}, bf16[192,2,1,96,128]{4,3,2,1,0:T(8,128)(2,1)}, u32[]{:S(2)}) copy-start(bf16[192,2,1,96,128]{4,3,2,1,0:T(8,128)(2,1)} %param.12) | copy-start | bytes 28311556
  28.0 11.1 %copy-start.1 = (bf16[16,1536]{1,0:T(8,128)(2,1)S(1)}, bf16[16,1536]{1,0:T(8,128)(2,1)}, u32[]{:S(2)}) copy-start(bf16[16,1536]{1,0:T(8,128)(2,1)} %param.8) | copy-start | bytes 147460
  28.1 25.5 %copy-start.2 = (s32[512]{0:T(512)S(1)}, s32[512]{0:T(512)}, u32[]{:S(2)}) copy-start(s32[512]{0:T(512)} %param.15) | copy-start | bytes 6148
  31.0 16.7 %all-to-all-start.1 = ((f32[8,16,192]{2,1,0:T(8,128)}), f32[8,16,192]{2,1,0:T(8,128)S(1)}, u32[]{:S(2)}, u32[]{:S(2)}) async-start(f32[8,16,192]{2,1,0:T(8,128)} %convolution_bitcast_fusion), calls=%async_computation.1 | async-start | bytes 262144 | tf_op jit(solution)/shard_map/all_to_all | solution.py:84
  48.6 16.7 %all-to-all-start.2 = ((f32[32,16,192]{2,1,0:T(8,128)}), f32[32,16,192]{2,1,0:T(8,128)S(1)}, u32[]{:S(2)}, u32[]{:S(2)}) async-start(f32[32,16,192]{2,1,0:T(8,128)} %broadcast_in_dim.47), calls=%async_computation.2 | async-start | bytes 1048576 | tf_op jit(solution)/shard_map/all_to_all | solution.py:17

commit v6 on v4

--- a/solution.py
+++ b/solution.py
@@ -3,12 +3,21 @@
 import jax
 import jax.numpy as jnp
 from jax import lax
+from jax.experimental import pallas as pl
 from jax.sharding import PartitionSpec as P
 
 HD = 96
 PAGE = 128
 MAXP = 128
 GROUP = 2
+
+
+def _project_kernel(x_ref, g_ref, w_ref, o_ref):
+    wide = x_ref[...].astype(jnp.float32)
+    scale = lax.rsqrt(jnp.mean(wide * wide, axis=1, keepdims=True) + 1e-05)
+    normed = (wide * scale * g_ref[...]).astype(jnp.bfloat16)
+    rows = jnp.dot(normed, w_ref[...], preferred_element_type=jnp.float32).astype(jnp.bfloat16)
+    o_ref[...] = jnp.broadcast_to(rows[None], o_ref.shape)
 
 
 def exchange(rows, axis):
@@ -24,14 +33,13 @@
     first_slot = lax.axis_index("req") * slot_count
     slot_ids = jnp.arange(slot_count, dtype=jnp.int32)
     hidden_wide = hidden.astype(jnp.float32)
-    normed = (
-        hidden_wide
-        * lax.rsqrt(jnp.mean(hidden_wide * hidden_wide, axis=1, keepdims=True) + 1e-05)
-        * norm_gain
-    ).astype(jnp.bfloat16)
     served = lax.dynamic_slice_in_dim(occupant, first_slot, slot_count)
-    own_rows = jnp.dot(normed, w_qkv, preferred_element_type=jnp.float32).astype(jnp.bfloat16)
-    every_row = exchange(own_rows, "req")
+    req_count = lax.axis_size("req")
+    sent_rows = pl.pallas_call(
+        _project_kernel,
+        out_shape=jax.ShapeDtypeStruct((req_count, slot_count, w_qkv.shape[1]), jnp.bfloat16),
+    )(hidden, norm_gain.reshape(1, -1), w_qkv)
+    every_row = lax.all_to_all(sent_rows, "req", 0, 0).reshape(-1, w_qkv.shape[1])
     slot_rows = jnp.take(every_row, served, axis=0)
     slot_rows = slot_rows.reshape(slot_count, kv_local, GROUP + 2, HD)
     queries = slot_rows[:, :, :GROUP]

time: 62.2 us -> 63.4 us (1.019)
  Pallas kernels: 0 us -> 2.42 us
  matrix products: 7.5 us -> 6.38 us
    all_to_all x2 -> x1, starting transfers between devices: 12.2 us -> 3.65 us  [exchange(): lax.all_to_all(sent, axis, 0, 0)]
    all_to_all x0 -> x1, starting transfers between devices: none -> 8.58 us  [per_device(): lax.all_to_all(sent_rows, 'req', 0, 0).reshape(-1, w_qkv.shape[1])]
    all_to_all x2 -> x1, waiting for transfers between devices: 14.1 us -> 8.56 us  [exchange(): lax.all_to_all(sent, axis, 0, 0)]
    all_to_all x0 -> x1, waiting for transfers between devices: none -> 5.51 us  [per_device(): lax.all_to_all(sent_rows, 'req', 0, 0).reshape(-1, w_qkv.shape[1])]
    pallas_call x0 -> x1, Pallas kernels: none -> 2.42 us  [per_device(): pl.pallas_call(_project_kernel, out_shape=jax.ShapeDtypeStruct((req_count...]
    reshape x0 -> x1, local copies, waits for them, and re-layouts: none -> 1.29 us  [per_device(): norm_gain.reshape(1, -1)]
    dot_general x1 -> x0, matrix products: 1.12 us -> none  [per_device(): jnp.dot(normed, w_qkv, preferred_element_type=jnp.float32)]
    reduce_sum x1 -> x0, other arithmetic: 1.02 us -> none  [per_device(): jnp.mean(hidden_wide * hidden_wide, axis=1, keepdims=True) + 1e-05]
where the time goes in v6:
time: 63.4 us; the launch traced here: 62.8 us
  waiting for transfers between devices  22.4 us (35%)
  starting transfers between devices  20.4 us (32%)
  other arithmetic  7.48 us (12%)
  matrix products  6.38 us (10%)
  local copies, waits for them, and re-layouts  3.63 us (6%)
  Pallas kernels  2.42 us (4%)
    all_to_all x1, starting transfers between devices, per_device(): lax.all_to_all(sent_rows, 'req', 0, 0).reshape(-1, w_qkv.shape[1])  8.58 us
    all_to_all x1, waiting for transfers between devices, exchange(): lax.all_to_all(sent, axis, 0, 0)  8.56 us
    all_to_all x1, waiting for transfers between devices, per_device(): summed = jnp.sum(lax.all_to_all(blocks, 'kv', 0, 0), axis=0)  8.29 us
    all_to_all x1, starting transfers between devices, per_device(): summed = jnp.sum(lax.all_to_all(blocks, 'kv', 0, 0), axis=0)  8.18 us
    all_to_all x1, waiting for transfers between devices, per_device(): lax.all_to_all(sent_rows, 'req', 0, 0).reshape(-1, w_qkv.shape[1])  5.51 us
    all_to_all x1, starting transfers between devices, exchange(): lax.all_to_all(sent, axis, 0, 0)  3.65 us
    dot_general x1, matrix products, per_device(): jnp.einsum('sgjd,pgdt->sgjpt', queries, cache_pages[:, 0], preferred_elem...  3.36 us
    pallas_call x1, Pallas kernels, per_device(): pl.pallas_call(_project_kernel, out_shape=jax.ShapeDtypeStruct((req_count...  2.42 us
  transfers between devices with their start and end apart: 3, of which 3 were waited for; matrix products, arithmetic and copies ran while one was open for 8% of the time, Pallas kernels for 0%

profile of v6, /device:TPU:1, one launch (start us, length us, event | category | flops | bytes accessed | tf_op | source)
XLA Modules:
  0.0 62.8 jit_solution(11799341913902025253)
XLA Ops:
  0.0 1.3 %reshape.221.g_ref = f32[1,1536]{1,0:T(1,128)} reshape(f32[1536]{0:T(1024)} %param.9) | data formatting | bytes 12288 | tf_op jit(solution)/shard_map/reshape | solution.py:41
  1.3 2.4 %shard_map.82 = bf16[32,16,384]{2,1,0:T(8,128)(2,1)} custom-call(bf16[16,1536]{1,0:T(8,128)(2,1)} %x_ref.1, f32[1,1536]{1,0:T(1,128)} %reshape.221.g_ref, bf16[1536,384]{1,0:T(8,128)(2,1)} %w_ref.1), custom_call_target="tpu_custom_call" | custom-call | tf_op jit(solution)/shard_map/pallas_call | solution.py:38
  3.7 8.6 %all-to-all-start = ((bf16[32,16,384]{2,1,0:T(8,128)(2,1)}), bf16[32,16,384]{2,1,0:T(8,128)(2,1)S(1)}, u32[]{:S(2)}, u32[]{:S(2)}) async-start(bf16[32,16,384]{2,1,0:T(8,128)(2,1)} %shard_map.82), calls=%async_computation | async-start | bytes 786432 | tf_op jit(solution)/shard_map/all_to_all | solution.py:42
  12.3 0.7 %and_select_fusion = s32[16]{0:T(128)S(1)} fusion(s32[16]{0:T(128)} %param.13), kind=kLoop, calls=%fused_computation.45 | loop fusion | flops 256 | bytes 128 | tf_op jit(solution)/shard_map/jit(floor_divide)/jit(_where)/select_n | solution.py:49
  13.0 0.1 iota_compare_fusion.2
  13.1 1.7 %select_reduce_fusion = (s32[192]{0:T(256)S(1)}, s32[16,192]{1,0:T(8,128)S(1)}) fusion(s32[16,128]{1,0:T(8,128)} %param.14, pred[16,128]{1,0:T(8,128)(4,1)S(1)} %iota_compare_fusion.2), kind=kLoop, calls=%fused_computation.13 | loop fusion | flops 2356032 | bytes 23296 | tf_op jit(solution)/shard_map/reduce_sum | solution.py:57
  14.7 0.7 %multiply_reduce_fusion.2 = (s32[192]{0:T(256)S(1)}, s32[192]{0:T(256)S(1)}) fusion(s32[16,192]{1,0:T(8,128)S(1)} %get-tuple-element.8, s32[16]{0:T(128)} %param.13), kind=kLoop, calls=%fused_computation.32 | loop fusion | flops 11904 | bytes 13888 | tf_op jit(solution)/shard_map/reduce_sum | solution.py:56
  15.5 0.1 iota_compare_fusion.1
  15.6 0.1 add_compare_fusion
  15.7 0.8 %compare_and_fusion = (pred[16]{0:T(512)(128)(4,1)S(1)}, s32[16]{0:T(128)S(1)}) fusion(s32[512]{0:T(512)} %param.15, s32[]{:T(128)S(6)} %select_n.32), kind=kLoop, calls=%fused_computation.44 | loop fusion | flops 96 | bytes 148 | tf_op jit(solution)/shard_map/jit(_take)/and | solution.py:43
  16.5 0.6 broadcast_and_fusion
  17.1 5.5 %all-to-all-done = bf16[32,16,384]{2,1,0:T(8,128)(2,1)S(1)} async-done(((bf16[32,16,384]{2,1,0:T(8,128)(2,1)}), bf16[32,16,384]{2,1,0:T(8,128)(2,1)S(1)}, u32[]{:S(2)}, u32[]{:S(2)}) %all-to-all-start) | async-done | bytes 393248 | tf_op jit(solution)/shard_map/all_to_all | solution.py:42
  22.6 0.6 gather_fusion
  23.2 0.1 gather.7
  23.3 0.1 copy_select_fusion
  23.3 0.1 multiply_reduce_fusion
  23.4 0.0 copy-start.2
  23.4 3.4 %fusion.8 = (f32[16,2]{0,1:T(2,128)S(1)}, f32[16,2,192,128]{3,0,2,1:T(8,128)S(1)}) fusion(pred[16,192,128]{2,0,1:T(8,128)(4,1)S(1)} %broadcast_and_fusion, bf16[192,2,1,96,128]{4,3,2,1,0:T(8,128)(2,1)} %param.12, bf16[16,1,4,96]{3,0,2,1:T(8,128)(2,1)S(1)} %copy_select_fusion), kind=kOutput, calls=%fused_computation.11 | convolution fusion | flops 153354208 | bytes 8265856 | tf_op jit(solution)/shard_map/sgjd,pgdt->sgjpt/dot_general | solution.py:63
  26.8 1.1 %fusion.6 = (f32[16,2]{0,1:T(2,128)S(1)}, bf16[16,1,2,192,128]{4,0,3,2,1:T(8,128)(2,1)S(1)}) fusion(f32[16,2,192,128]{3,0,2,1:T(8,128)S(1)} %get-tuple-element.16, f32[16,2]{0,1:T(2,128)S(1)} %multiply_maximum_fusion, pred[16,192,128]{2,0,1:T(8,128)(4,1)S(1)} %broadcast_and_fusion), kind=kLoop, calls=%fused_computation.9 | loop fusion | flops 3932128 | bytes 5112064 | tf_op jit(solution)/shard_map/reduce_sum | solution.py:78
  28.0 0.6 copy-done.2
  28.6 0.0 copy-start
  28.6 0.0 copy-start.1
  28.6 1.8 %fusion.27 = bf16[16,1,2,96]{3,0,2,1:T(8,128)(2,1)S(1)} fusion(bf16[192,2,1,96,128]{4,3,2,1,0:T(8,128)(2,1)S(1)} %copy-done.2, bf16[16,1,2,192,128]{4,0,3,2,1:T(8,128)(2,1)S(1)} %get-tuple-element.12, f32[16,2]{0,1:T(2,128)S(1)} %exponential_add_fusion, f32[16,96]{1,0:T(8,128)S(1)} %get-tuple-element.13, f32[16,2]{0,1:T(2,128)S(1)} %bitcast_convert_fusion), kind=kOutput, calls=%fused_computation.23 | convolution fusion | flops 151007232 | bytes 6307840 | tf_op jit(solution)/shard_map/sgjpt,pgdt->sgjd/dot_general | solution.py:79
  30.4 0.1 broadcast_in_dim.33
  30.5 0.7 %broadcast_in_dim.34 = bf16[32,16,192]{2,1,0:T(8,128)(2,1)} broadcast(bf16[16,192]{1,0:T(8,128)(2,1)S(1)} %broadcast_in_dim.33), dimensions={1,2} | broadcast | bytes 202752 | tf_op jit(solution)/shard_map/broadcast_in_dim | solution.py:25
  31.2 3.7 %all-to-all-start.1 = ((bf16[32,16,192]{2,1,0:T(8,128)(2,1)}), bf16[32,16,192]{2,1,0:T(8,128)(2,1)S(1)}, u32[]{:S(2)}, u32[]{:S(2)}) async-start(bf16[32,16,192]{2,1,0:T(8,128)(2,1)} %broadcast_in_dim.34), calls=%async_computation.1 | async-start | bytes 524288 | tf_op jit(solution)/shard_map/all_to_all | solution.py:26
  34.9 0.0 copy-done
  34.9 0.3 copy.24
  35.2 8.6 %all-to-all-done.1 = bf16[32,16,192]{2,1,0:T(8,128)(2,1)S(1)} async-done(((bf16[32,16,192]{2,1,0:T(8,128)(2,1)}), bf16[32,16,192]{2,1,0:T(8,128)(2,1)S(1)}, u32[]{:S(2)}, u32[]{:S(2)}) %all-to-all-start.1) | async-done | bytes 196640 | tf_op jit(solution)/shard_map/all_to_all | solution.py:26
  43.8 0.0 copy-done.1
  43.8 1.2 %convolution_bitcast_fusion = f32[8,16,192]{2,1,0:T(8,128)} fusion(bf16[8,192,192]{2,1,0:T(8,128)(2,1)S(1)} %bitcast.100, bf16[512,192]{1,0:T(8,128)(2,1)S(1)} %bitcast.101, s32[512]{0:T(512)S(1)} %copy-done.1, s32[16]{0:T(128)S(1)} %iota_add_fusion), kind=kOutput, calls=%fused_computation.17 | convolution fusion | flops 12594176 | bytes 886848 | tf_op jit(solution)/shard_map/sa,kca->ksc/dot_general | solution.py:90
  44.9 8.2 %all-to-all-start.2 = ((f32[8,16,192]{2,1,0:T(8,128)}), f32[8,16,192]{2,1,0:T(8,128)S(1)}, u32[]{:S(2)}, u32[]{:S(2)}) async-start(f32[8,16,192]{2,1,0:T(8,128)} %convolution_bitcast_fusion), calls=%async_computation.2 | async-start | bytes 262144 | tf_op jit(solution)/shard_map/all_to_all | solution.py:96
  53.1 8.3 %all-to-all-done.2 = f32[8,16,192]{2,1,0:T(8,128)S(1)} async-done(((f32[8,16,192]{2,1,0:T(8,128)}), f32[8,16,192]{2,1,0:T(8,128)S(1)}, u32[]{:S(2)}, u32[]{:S(2)}) %all-to-all-start.2) | async-done | bytes 98336 | tf_op jit(solution)/shard_map/all_to_all | solution.py:96
  61.4 1.4 %add_convert_fusion = bf16[16,192]{1,0:T(8,128)(2,1)} fusion(f32[16,192]{1,0:T(8,128)S(1)} %reduce_sum.69, bf16[16,1536]{1,0:T(8,128)(2,1)} %x_ref.1, s32[]{:T(128)S(6)} %select_n.30), kind=kLoop, calls=%fused_computation.29 | loop fusion | flops 9216 | bytes 24580 | tf_op jit(solution)/shard_map/convert_element_type | solution.py:98
  (10 shorter events, 0.1 us)
Async XLA Ops:
  3.7 18.9 %all-to-all-start = ((bf16[32,16,384]{2,1,0:T(8,128)(2,1)}), bf16[32,16,384]{2,1,0:T(8,128)(2,1)S(1)}, u32[]{:S(2)}, u32[]{:S(2)}) async-start(bf16[32,16,384]{2,1,0:T(8,128)(2,1)} %shard_map.82), calls=%async_computation | async-start | bytes 786432 | tf_op jit(solution)/shard_map/all_to_all | solution.py:42
  23.4 5.1 %copy-start.2 = (bf16[192,2,1,96,128]{4,3,2,1,0:T(8,128)(2,1)S(1)}, bf16[192,2,1,96,128]{4,3,2,1,0:T(8,128)(2,1)}, u32[]{:S(2)}) copy-start(bf16[192,2,1,96,128]{4,3,2,1,0:T(8,128)(2,1)} %param.12) | copy-start | bytes 28311556
  28.6 6.3 %copy-start = (bf16[1536,192]{0,1:T(8,128)(2,1)S(1)}, bf16[1536,192]{0,1:T(8,128)(2,1)}, u32[]{:S(2)}) copy-start(bf16[1536,192]{0,1:T(8,128)(2,1)} %param.11) | copy-start | bytes 1769476
  28.6 15.2 %copy-start.1 = (s32[512]{0:T(512)S(1)}, s32[512]{0:T(512)}, u32[]{:S(2)}) copy-start(s32[512]{0:T(512)} %param.15) | copy-start | bytes 6148
  31.2 12.5 %all-to-all-start.1 = ((bf16[32,16,192]{2,1,0:T(8,128)(2,1)}), bf16[32,16,192]{2,1,0:T(8,128)(2,1)S(1)}, u32[]{:S(2)}, u32[]{:S(2)}) async-start(bf16[32,16,192]{2,1,0:T(8,128)(2,1)} %broadcast_in_dim.34), calls=%async_computation.1 | async-start | bytes 524288 | tf_op jit(solution)/shard_map/all_to_all | solution.py:26
  44.9 16.5 %all-to-all-start.2 = ((f32[8,16,192]{2,1,0:T(8,128)}), f32[8,16,192]{2,1,0:T(8,128)S(1)}, u32[]{:S(2)}, u32[]{:S(2)}) async-start(f32[8,16,192]{2,1,0:T(8,128)} %convolution_bitcast_fusion), calls=%async_computation.2 | async-start | bytes 262144 | tf_op jit(solution)/shard_map/all_to_all | solution.py:96

commit v7 on v6

--- a/solution.py
+++ b/solution.py
@@ -38,7 +38,7 @@
     sent_rows = pl.pallas_call(
         _project_kernel,
         out_shape=jax.ShapeDtypeStruct((req_count, slot_count, w_qkv.shape[1]), jnp.bfloat16),
-    )(hidden, norm_gain.reshape(1, -1), w_qkv)
+    )(hidden, norm_gain, w_qkv)
     every_row = lax.all_to_all(sent_rows, "req", 0, 0).reshape(-1, w_qkv.shape[1])
     slot_rows = jnp.take(every_row, served, axis=0)
     slot_rows = slot_rows.reshape(slot_count, kv_local, GROUP + 2, HD)

time: 63.4 us -> 62 us (0.978)
  local copies, waits for them, and re-layouts: 3.63 us -> 2.34 us
    reshape x1 -> x0, local copies, waits for them, and re-layouts: 1.29 us -> none  [per_device(): norm_gain.reshape(1, -1)]
where the time goes in v7:
time: 62 us; the launch traced here: 61.5 us
  waiting for transfers between devices  22.4 us (36%)
  starting transfers between devices  20.4 us (33%)
  other arithmetic  7.48 us (12%)
  matrix products  6.37 us (10%)
  Pallas kernels  2.42 us (4%)
  local copies, waits for them, and re-layouts  2.34 us (4%)
    all_to_all x1, starting transfers between devices, per_device(): lax.all_to_all(sent_rows, 'req', 0, 0).reshape(-1, w_qkv.shape[1])  8.58 us
    all_to_all x1, waiting for transfers between devices, exchange(): lax.all_to_all(sent, axis, 0, 0)  8.56 us
    all_to_all x1, waiting for transfers between devices, per_device(): summed = jnp.sum(lax.all_to_all(blocks, 'kv', 0, 0), axis=0)  8.29 us
    all_to_all x1, starting transfers between devices, per_device(): summed = jnp.sum(lax.all_to_all(blocks, 'kv', 0, 0), axis=0)  8.19 us
    all_to_all x1, waiting for transfers between devices, per_device(): lax.all_to_all(sent_rows, 'req', 0, 0).reshape(-1, w_qkv.shape[1])  5.51 us
    all_to_all x1, starting transfers between devices, exchange(): lax.all_to_all(sent, axis, 0, 0)  3.65 us
    dot_general x1, matrix products, per_device(): jnp.einsum('sgjd,pgdt->sgjpt', queries, cache_pages[:, 0], preferred_elem...  3.36 us
    pallas_call x1, Pallas kernels, per_device(): pl.pallas_call(_project_kernel, out_shape=jax.ShapeDtypeStruct((req_count...  2.42 us
  transfers between devices with their start and end apart: 3, of which 3 were waited for; matrix products, arithmetic and copies ran while one was open for 8% of the time, Pallas kernels for 0%

profile of v7, /device:TPU:1, one launch (start us, length us, event | category | flops | bytes accessed | tf_op | source)
XLA Modules:
  0.0 61.5 jit_solution(17542134186326924485)
XLA Ops:
  0.0 2.4 %shard_map.82 = bf16[32,16,384]{2,1,0:T(8,128)(2,1)} custom-call(bf16[16,1536]{1,0:T(8,128)(2,1)} %x_ref.1, f32[1536]{0:T(1024)} %g_ref.1, bf16[1536,384]{1,0:T(8,128)(2,1)} %w_ref.1), custom_call_target="tpu_custom_call" | custom-call | tf_op jit(solution)/shard_map/pallas_call | solution.py:38
  2.4 8.6 %all-to-all-start = ((bf16[32,16,384]{2,1,0:T(8,128)(2,1)}), bf16[32,16,384]{2,1,0:T(8,128)(2,1)S(1)}, u32[]{:S(2)}, u32[]{:S(2)}) async-start(bf16[32,16,384]{2,1,0:T(8,128)(2,1)} %shard_map.82), calls=%async_computation | async-start | bytes 786432 | tf_op jit(solution)/shard_map/all_to_all | solution.py:42
  11.0 0.7 %and_select_fusion = s32[16]{0:T(128)S(1)} fusion(s32[16]{0:T(128)} %param.13), kind=kLoop, calls=%fused_computation.45 | loop fusion | flops 256 | bytes 128 | tf_op jit(solution)/shard_map/jit(floor_divide)/jit(_where)/select_n | solution.py:49
  11.7 0.1 iota_compare_fusion.2
  11.8 1.7 %select_reduce_fusion = (s32[192]{0:T(256)S(1)}, s32[16,192]{1,0:T(8,128)S(1)}) fusion(s32[16,128]{1,0:T(8,128)} %param.14, pred[16,128]{1,0:T(8,128)(4,1)S(1)} %iota_compare_fusion.2), kind=kLoop, calls=%fused_computation.13 | loop fusion | flops 2356032 | bytes 23296 | tf_op jit(solution)/shard_map/reduce_sum | solution.py:57
  13.4 0.7 %multiply_reduce_fusion.2 = (s32[192]{0:T(256)S(1)}, s32[192]{0:T(256)S(1)}) fusion(s32[16,192]{1,0:T(8,128)S(1)} %get-tuple-element.8, s32[16]{0:T(128)} %param.13), kind=kLoop, calls=%fused_computation.32 | loop fusion | flops 11904 | bytes 13888 | tf_op jit(solution)/shard_map/reduce_sum | solution.py:56
  14.2 0.1 iota_compare_fusion.1
  14.3 0.1 add_compare_fusion
  14.4 0.8 %compare_and_fusion = (pred[16]{0:T(512)(128)(4,1)S(1)}, s32[16]{0:T(128)S(1)}) fusion(s32[512]{0:T(512)} %param.15, s32[]{:T(128)S(6)} %select_n.32), kind=kLoop, calls=%fused_computation.44 | loop fusion | flops 96 | bytes 148 | tf_op jit(solution)/shard_map/jit(_take)/and | solution.py:43
  15.2 0.6 broadcast_and_fusion
  15.8 5.5 %all-to-all-done = bf16[32,16,384]{2,1,0:T(8,128)(2,1)S(1)} async-done(((bf16[32,16,384]{2,1,0:T(8,128)(2,1)}), bf16[32,16,384]{2,1,0:T(8,128)(2,1)S(1)}, u32[]{:S(2)}, u32[]{:S(2)}) %all-to-all-start) | async-done | bytes 393248 | tf_op jit(solution)/shard_map/all_to_all | solution.py:42
  21.3 0.6 gather_fusion
  21.9 0.1 gather.7
  22.0 0.1 copy_select_fusion
  22.1 0.1 multiply_reduce_fusion
  22.1 0.0 copy-start.2
  22.1 3.4 %fusion.8 = (f32[16,2]{0,1:T(2,128)S(1)}, f32[16,2,192,128]{3,0,2,1:T(8,128)S(1)}) fusion(pred[16,192,128]{2,0,1:T(8,128)(4,1)S(1)} %broadcast_and_fusion, bf16[192,2,1,96,128]{4,3,2,1,0:T(8,128)(2,1)} %param.12, bf16[16,1,4,96]{3,0,2,1:T(8,128)(2,1)S(1)} %copy_select_fusion), kind=kOutput, calls=%fused_computation.11 | convolution fusion | flops 153354208 | bytes 8265856 | tf_op jit(solution)/shard_map/sgjd,pgdt->sgjpt/dot_general | solution.py:63
  25.5 1.1 %fusion.6 = (f32[16,2]{0,1:T(2,128)S(1)}, bf16[16,1,2,192,128]{4,0,3,2,1:T(8,128)(2,1)S(1)}) fusion(f32[16,2,192,128]{3,0,2,1:T(8,128)S(1)} %get-tuple-element.16, f32[16,2]{0,1:T(2,128)S(1)} %multiply_maximum_fusion, pred[16,192,128]{2,0,1:T(8,128)(4,1)S(1)} %broadcast_and_fusion), kind=kLoop, calls=%fused_computation.9 | loop fusion | flops 3932128 | bytes 5112064 | tf_op jit(solution)/shard_map/reduce_sum | solution.py:78
  26.7 0.6 copy-done.2
  27.3 0.0 copy-start
  27.3 0.0 copy-start.1
  27.3 1.8 %fusion.27 = bf16[16,1,2,96]{3,0,2,1:T(8,128)(2,1)S(1)} fusion(bf16[192,2,1,96,128]{4,3,2,1,0:T(8,128)(2,1)S(1)} %copy-done.2, bf16[16,1,2,192,128]{4,0,3,2,1:T(8,128)(2,1)S(1)} %get-tuple-element.12, f32[16,2]{0,1:T(2,128)S(1)} %exponential_add_fusion, f32[16,96]{1,0:T(8,128)S(1)} %get-tuple-element.13, f32[16,2]{0,1:T(2,128)S(1)} %bitcast_convert_fusion), kind=kOutput, calls=%fused_computation.23 | convolution fusion | flops 151007232 | bytes 6307840 | tf_op jit(solution)/shard_map/sgjpt,pgdt->sgjd/dot_general | solution.py:79
  29.1 0.1 broadcast_in_dim.33
  29.2 0.7 %broadcast_in_dim.34 = bf16[32,16,192]{2,1,0:T(8,128)(2,1)} broadcast(bf16[16,192]{1,0:T(8,128)(2,1)S(1)} %broadcast_in_dim.33), dimensions={1,2} | broadcast | bytes 202752 | tf_op jit(solution)/shard_map/broadcast_in_dim | solution.py:25
  29.9 3.7 %all-to-all-start.1 = ((bf16[32,16,192]{2,1,0:T(8,128)(2,1)}), bf16[32,16,192]{2,1,0:T(8,128)(2,1)S(1)}, u32[]{:S(2)}, u32[]{:S(2)}) async-start(bf16[32,16,192]{2,1,0:T(8,128)(2,1)} %broadcast_in_dim.34), calls=%async_computation.1 | async-start | bytes 524288 | tf_op jit(solution)/shard_map/all_to_all | solution.py:26
  33.6 0.0 copy-done
  33.6 0.3 copy.24
  33.9 8.6 %all-to-all-done.1 = bf16[32,16,192]{2,1,0:T(8,128)(2,1)S(1)} async-done(((bf16[32,16,192]{2,1,0:T(8,128)(2,1)}), bf16[32,16,192]{2,1,0:T(8,128)(2,1)S(1)}, u32[]{:S(2)}, u32[]{:S(2)}) %all-to-all-start.1) | async-done | bytes 196640 | tf_op jit(solution)/shard_map/all_to_all | solution.py:26
  42.5 0.0 copy-done.1
  42.5 1.2 %convolution_bitcast_fusion = f32[8,16,192]{2,1,0:T(8,128)} fusion(bf16[8,192,192]{2,1,0:T(8,128)(2,1)S(1)} %bitcast.100, bf16[512,192]{1,0:T(8,128)(2,1)S(1)} %bitcast.101, s32[512]{0:T(512)S(1)} %copy-done.1, s32[16]{0:T(128)S(1)} %iota_add_fusion), kind=kOutput, calls=%fused_computation.17 | convolution fusion | flops 12594176 | bytes 886848 | tf_op jit(solution)/shard_map/sa,kca->ksc/dot_general | solution.py:90
  43.6 8.2 %all-to-all-start.2 = ((f32[8,16,192]{2,1,0:T(8,128)}), f32[8,16,192]{2,1,0:T(8,128)S(1)}, u32[]{:S(2)}, u32[]{:S(2)}) async-start(f32[8,16,192]{2,1,0:T(8,128)} %convolution_bitcast_fusion), calls=%async_computation.2 | async-start | bytes 262144 | tf_op jit(solution)/shard_map/all_to_all | solution.py:96
  51.8 8.3 %all-to-all-done.2 = f32[8,16,192]{2,1,0:T(8,128)S(1)} async-done(((f32[8,16,192]{2,1,0:T(8,128)}), f32[8,16,192]{2,1,0:T(8,128)S(1)}, u32[]{:S(2)}, u32[]{:S(2)}) %all-to-all-start.2) | async-done | bytes 98336 | tf_op jit(solution)/shard_map/all_to_all | solution.py:96
  60.1 1.4 %add_convert_fusion = bf16[16,192]{1,0:T(8,128)(2,1)} fusion(f32[16,192]{1,0:T(8,128)S(1)} %reduce_sum.69, bf16[16,1536]{1,0:T(8,128)(2,1)} %x_ref.1, s32[]{:T(128)S(6)} %select_n.30), kind=kLoop, calls=%fused_computation.29 | loop fusion | flops 9216 | bytes 24580 | tf_op jit(solution)/shard_map/convert_element_type | solution.py:98
  (10 shorter events, 0.1 us)
Async XLA Ops:
  2.4 18.9 %all-to-all-start = ((bf16[32,16,384]{2,1,0:T(8,128)(2,1)}), bf16[32,16,384]{2,1,0:T(8,128)(2,1)S(1)}, u32[]{:S(2)}, u32[]{:S(2)}) async-start(bf16[32,16,384]{2,1,0:T(8,128)(2,1)} %shard_map.82), calls=%async_computation | async-start | bytes 786432 | tf_op jit(solution)/shard_map/all_to_all | solution.py:42
  22.1 5.1 %copy-start.2 = (bf16[192,2,1,96,128]{4,3,2,1,0:T(8,128)(2,1)S(1)}, bf16[192,2,1,96,128]{4,3,2,1,0:T(8,128)(2,1)}, u32[]{:S(2)}) copy-start(bf16[192,2,1,96,128]{4,3,2,1,0:T(8,128)(2,1)} %param.12) | copy-start | bytes 28311556
  27.3 6.3 %copy-start = (bf16[1536,192]{0,1:T(8,128)(2,1)S(1)}, bf16[1536,192]{0,1:T(8,128)(2,1)}, u32[]{:S(2)}) copy-start(bf16[1536,192]{0,1:T(8,128)(2,1)} %param.11) | copy-start | bytes 1769476
  27.3 15.2 %copy-start.1 = (s32[512]{0:T(512)S(1)}, s32[512]{0:T(512)}, u32[]{:S(2)}) copy-start(s32[512]{0:T(512)} %param.15) | copy-start | bytes 6148
  29.9 12.5 %all-to-all-start.1 = ((bf16[32,16,192]{2,1,0:T(8,128)(2,1)}), bf16[32,16,192]{2,1,0:T(8,128)(2,1)S(1)}, u32[]{:S(2)}, u32[]{:S(2)}) async-start(bf16[32,16,192]{2,1,0:T(8,128)(2,1)} %broadcast_in_dim.34), calls=%async_computation.1 | async-start | bytes 524288 | tf_op jit(solution)/shard_map/all_to_all | solution.py:26
  43.6 16.5 %all-to-all-start.2 = ((f32[8,16,192]{2,1,0:T(8,128)}), f32[8,16,192]{2,1,0:T(8,128)S(1)}, u32[]{:S(2)}, u32[]{:S(2)}) async-start(f32[8,16,192]{2,1,0:T(8,128)} %convolution_bitcast_fusion), calls=%async_computation.2 | async-start | bytes 262144 | tf_op jit(solution)/shard_map/all_to_all | solution.py:96

commit v8 on v7

--- a/solution.py
+++ b/solution.py
@@ -95,6 +95,7 @@
     )
     summed = jnp.sum(lax.all_to_all(blocks, "kv", 0, 0), axis=0)
     residual = lax.dynamic_slice_in_dim(hidden_wide, lax.axis_index("kv") * col_share, col_share, 1)
+    residual = lax.optimization_barrier(residual)
     return (residual + summed).astype(jnp.bfloat16)
 
 

time: 62 us -> 61.3 us (0.989)
  waiting for transfers between devices: 22.4 us -> 21.6 us
    convert_element_type x1, other arithmetic: 1.39 us -> 0.6 us  [per_device(): return (residual + summed).astype(jnp.bfloat16)]
    all_to_all x1, waiting for transfers between devices: 8.29 us -> 7.51 us  [per_device(): summed = jnp.sum(lax.all_to_all(blocks, 'kv', 0, 0), axis=0)]
    convert_element_type x0 -> x1, other arithmetic: none -> 0.78 us  [per_device(): hidden_wide = hidden.astype(jnp.float32)]
  transfers between devices with their start and end apart: 3 -> 3, of which waited for: 3 -> 3; matrix products, arithmetic and copies ran while one was open for 8% -> 10% of each run, Pallas kernels for 0% -> 0%
where the time goes in v8:
time: 61.3 us; the launch traced here: 60.7 us
  waiting for transfers between devices  21.6 us (35%)
  starting transfers between devices  20.4 us (33%)
  other arithmetic  7.48 us (12%)
  matrix products  6.37 us (10%)
  Pallas kernels  2.42 us (4%)
  local copies, waits for them, and re-layouts  2.34 us (4%)
    all_to_all x1, starting transfers between devices, per_device(): lax.all_to_all(sent_rows, 'req', 0, 0).reshape(-1, w_qkv.shape[1])  8.58 us
    all_to_all x1, waiting for transfers between devices, exchange(): lax.all_to_all(sent, axis, 0, 0)  8.56 us
    all_to_all x1, starting transfers between devices, per_device(): summed = jnp.sum(lax.all_to_all(blocks, 'kv', 0, 0), axis=0)  8.19 us
    all_to_all x1, waiting for transfers between devices, per_device(): summed = jnp.sum(lax.all_to_all(blocks, 'kv', 0, 0), axis=0)  7.51 us
    all_to_all x1, waiting for transfers between devices, per_device(): lax.all_to_all(sent_rows, 'req', 0, 0).reshape(-1, w_qkv.shape[1])  5.51 us
    all_to_all x1, starting transfers between devices, exchange(): lax.all_to_all(sent, axis, 0, 0)  3.65 us
    dot_general x1, matrix products, per_device(): jnp.einsum('sgjd,pgdt->sgjpt', queries, cache_pages[:, 0], preferred_elem...  3.36 us
    pallas_call x1, Pallas kernels, per_device(): pl.pallas_call(_project_kernel, out_shape=jax.ShapeDtypeStruct((req_count...  2.42 us
  transfers between devices with their start and end apart: 3, of which 3 were waited for; matrix products, arithmetic and copies ran while one was open for 10% of the time, Pallas kernels for 0%

profile of v8, /device:TPU:1, one launch (start us, length us, event | category | flops | bytes accessed | tf_op | source)
XLA Modules:
  0.0 60.7 jit_solution(14569084863057892118)
XLA Ops:
  0.0 2.4 %shard_map.82 = bf16[32,16,384]{2,1,0:T(8,128)(2,1)} custom-call(bf16[16,1536]{1,0:T(8,128)(2,1)} %x_ref.1, f32[1536]{0:T(1024)} %g_ref.1, bf16[1536,384]{1,0:T(8,128)(2,1)} %w_ref.1), custom_call_target="tpu_custom_call" | custom-call | tf_op jit(solution)/shard_map/pallas_call | solution.py:38
  2.4 8.6 %all-to-all-start = ((bf16[32,16,384]{2,1,0:T(8,128)(2,1)}), bf16[32,16,384]{2,1,0:T(8,128)(2,1)S(1)}, u32[]{:S(2)}, u32[]{:S(2)}) async-start(bf16[32,16,384]{2,1,0:T(8,128)(2,1)} %shard_map.82), calls=%async_computation | async-start | bytes 786432 | tf_op jit(solution)/shard_map/all_to_all | solution.py:42
  11.0 0.7 %and_select_fusion = s32[16]{0:T(128)S(1)} fusion(s32[16]{0:T(128)} %param.13), kind=kLoop, calls=%fused_computation.46 | loop fusion | flops 256 | bytes 128 | tf_op jit(solution)/shard_map/jit(floor_divide)/jit(_where)/select_n | solution.py:49
  11.7 0.1 iota_compare_fusion.2
  11.8 1.7 %select_reduce_fusion = (s32[192]{0:T(256)S(1)}, s32[16,192]{1,0:T(8,128)S(1)}) fusion(s32[16,128]{1,0:T(8,128)} %param.14, pred[16,128]{1,0:T(8,128)(4,1)S(1)} %iota_compare_fusion.2), kind=kLoop, calls=%fused_computation.13 | loop fusion | flops 2356032 | bytes 23296 | tf_op jit(solution)/shard_map/reduce_sum | solution.py:57
  13.4 0.7 %multiply_reduce_fusion.2 = (s32[192]{0:T(256)S(1)}, s32[192]{0:T(256)S(1)}) fusion(s32[16,192]{1,0:T(8,128)S(1)} %get-tuple-element.8, s32[16]{0:T(128)} %param.13), kind=kLoop, calls=%fused_computation.32 | loop fusion | flops 11904 | bytes 13888 | tf_op jit(solution)/shard_map/reduce_sum | solution.py:56
  14.2 0.1 iota_compare_fusion.1
  14.3 0.1 add_compare_fusion
  14.4 0.8 %compare_and_fusion = (pred[16]{0:T(512)(128)(4,1)S(1)}, s32[16]{0:T(128)S(1)}) fusion(s32[512]{0:T(512)} %param.15, s32[]{:T(128)S(6)} %select_n.32), kind=kLoop, calls=%fused_computation.45 | loop fusion | flops 96 | bytes 148 | tf_op jit(solution)/shard_map/jit(_take)/and | solution.py:43
  15.2 0.6 broadcast_and_fusion
  15.8 5.5 %all-to-all-done = bf16[32,16,384]{2,1,0:T(8,128)(2,1)S(1)} async-done(((bf16[32,16,384]{2,1,0:T(8,128)(2,1)}), bf16[32,16,384]{2,1,0:T(8,128)(2,1)S(1)}, u32[]{:S(2)}, u32[]{:S(2)}) %all-to-all-start) | async-done | bytes 393248 | tf_op jit(solution)/shard_map/all_to_all | solution.py:42
  21.3 0.6 gather_fusion
  21.9 0.1 gather.7
  22.0 0.1 copy_select_fusion
  22.1 0.1 multiply_reduce_fusion
  22.1 0.0 copy-start.2
  22.1 3.4 %fusion.8 = (f32[16,2]{0,1:T(2,128)S(1)}, f32[16,2,192,128]{3,0,2,1:T(8,128)S(1)}) fusion(pred[16,192,128]{2,0,1:T(8,128)(4,1)S(1)} %broadcast_and_fusion, bf16[192,2,1,96,128]{4,3,2,1,0:T(8,128)(2,1)} %param.12, bf16[16,1,4,96]{3,0,2,1:T(8,128)(2,1)S(1)} %copy_select_fusion), kind=kOutput, calls=%fused_computation.11 | convolution fusion | flops 153354208 | bytes 8265856 | tf_op jit(solution)/shard_map/sgjd,pgdt->sgjpt/dot_general | solution.py:63
  25.5 1.1 %fusion.6 = (f32[16,2]{0,1:T(2,128)S(1)}, bf16[16,1,2,192,128]{4,0,3,2,1:T(8,128)(2,1)S(1)}) fusion(f32[16,2,192,128]{3,0,2,1:T(8,128)S(1)} %get-tuple-element.16, f32[16,2]{0,1:T(2,128)S(1)} %multiply_maximum_fusion, pred[16,192,128]{2,0,1:T(8,128)(4,1)S(1)} %broadcast_and_fusion), kind=kLoop, calls=%fused_computation.9 | loop fusion | flops 3932128 | bytes 5112064 | tf_op jit(solution)/shard_map/reduce_sum | solution.py:78
  26.7 0.6 copy-done.2
  27.3 0.0 copy-start
  27.3 0.0 copy-start.1
  27.3 1.8 %fusion.27 = bf16[16,1,2,96]{3,0,2,1:T(8,128)(2,1)S(1)} fusion(bf16[192,2,1,96,128]{4,3,2,1,0:T(8,128)(2,1)S(1)} %copy-done.2, bf16[16,1,2,192,128]{4,0,3,2,1:T(8,128)(2,1)S(1)} %get-tuple-element.12, f32[16,2]{0,1:T(2,128)S(1)} %exponential_add_fusion, f32[16,96]{1,0:T(8,128)S(1)} %get-tuple-element.13, f32[16,2]{0,1:T(2,128)S(1)} %bitcast_convert_fusion), kind=kOutput, calls=%fused_computation.23 | convolution fusion | flops 151007232 | bytes 6307840 | tf_op jit(solution)/shard_map/sgjpt,pgdt->sgjd/dot_general | solution.py:79
  29.1 0.1 broadcast_in_dim.33
  29.2 0.7 %broadcast_in_dim.34 = bf16[32,16,192]{2,1,0:T(8,128)(2,1)} broadcast(bf16[16,192]{1,0:T(8,128)(2,1)S(1)} %broadcast_in_dim.33), dimensions={1,2} | broadcast | bytes 202752 | tf_op jit(solution)/shard_map/broadcast_in_dim | solution.py:25
  29.9 3.7 %all-to-all-start.1 = ((bf16[32,16,192]{2,1,0:T(8,128)(2,1)}), bf16[32,16,192]{2,1,0:T(8,128)(2,1)S(1)}, u32[]{:S(2)}, u32[]{:S(2)}) async-start(bf16[32,16,192]{2,1,0:T(8,128)(2,1)} %broadcast_in_dim.34), calls=%async_computation.1 | async-start | bytes 524288 | tf_op jit(solution)/shard_map/all_to_all | solution.py:26
  33.6 0.0 copy-done
  33.6 0.3 copy.24
  33.9 8.6 %all-to-all-done.1 = bf16[32,16,192]{2,1,0:T(8,128)(2,1)S(1)} async-done(((bf16[32,16,192]{2,1,0:T(8,128)(2,1)}), bf16[32,16,192]{2,1,0:T(8,128)(2,1)S(1)}, u32[]{:S(2)}, u32[]{:S(2)}) %all-to-all-start.1) | async-done | bytes 196640 | tf_op jit(solution)/shard_map/all_to_all | solution.py:26
  42.5 0.0 copy-done.1
  42.5 1.2 %convolution_bitcast_fusion = f32[8,16,192]{2,1,0:T(8,128)} fusion(bf16[8,192,192]{2,1,0:T(8,128)(2,1)S(1)} %bitcast.100, bf16[512,192]{1,0:T(8,128)(2,1)S(1)} %bitcast.101, s32[512]{0:T(512)S(1)} %copy-done.1, s32[16]{0:T(128)S(1)} %iota_add_fusion), kind=kOutput, calls=%fused_computation.17 | convolution fusion | flops 12594176 | bytes 886848 | tf_op jit(solution)/shard_map/sa,kca->ksc/dot_general | solution.py:90
  43.6 8.2 %all-to-all-start.2 = ((f32[8,16,192]{2,1,0:T(8,128)}), f32[8,16,192]{2,1,0:T(8,128)S(1)}, u32[]{:S(2)}, u32[]{:S(2)}) async-start(f32[8,16,192]{2,1,0:T(8,128)} %convolution_bitcast_fusion), calls=%async_computation.2 | async-start | bytes 262144 | tf_op jit(solution)/shard_map/all_to_all | solution.py:96
  51.8 0.8 %dynamic-slice_convert_fusion = f32[16,192]{1,0:T(8,128)S(1)} fusion(bf16[16,1536]{1,0:T(8,128)(2,1)} %x_ref.1, s32[]{:T(128)S(6)} %select_n.30), kind=kLoop, calls=%fused_computation.35 | loop fusion | flops 3072 | bytes 18436 | tf_op jit(solution)/shard_map/convert_element_type | solution.py:35
  52.6 7.5 %all-to-all-done.2 = f32[8,16,192]{2,1,0:T(8,128)S(1)} async-done(((f32[8,16,192]{2,1,0:T(8,128)}), f32[8,16,192]{2,1,0:T(8,128)S(1)}, u32[]{:S(2)}, u32[]{:S(2)}) %all-to-all-start.2) | async-done | bytes 98336 | tf_op jit(solution)/shard_map/all_to_all | solution.py:96
  60.1 0.6 add_convert_fusion
  (10 shorter events, 0.1 us)
Async XLA Ops:
  2.4 18.9 %all-to-all-start = ((bf16[32,16,384]{2,1,0:T(8,128)(2,1)}), bf16[32,16,384]{2,1,0:T(8,128)(2,1)S(1)}, u32[]{:S(2)}, u32[]{:S(2)}) async-start(bf16[32,16,384]{2,1,0:T(8,128)(2,1)} %shard_map.82), calls=%async_computation | async-start | bytes 786432 | tf_op jit(solution)/shard_map/all_to_all | solution.py:42
  22.1 5.1 %copy-start.2 = (bf16[192,2,1,96,128]{4,3,2,1,0:T(8,128)(2,1)S(1)}, bf16[192,2,1,96,128]{4,3,2,1,0:T(8,128)(2,1)}, u32[]{:S(2)}) copy-start(bf16[192,2,1,96,128]{4,3,2,1,0:T(8,128)(2,1)} %param.12) | copy-start | bytes 28311556
  27.3 6.3 %copy-start = (bf16[1536,192]{0,1:T(8,128)(2,1)S(1)}, bf16[1536,192]{0,1:T(8,128)(2,1)}, u32[]{:S(2)}) copy-start(bf16[1536,192]{0,1:T(8,128)(2,1)} %param.11) | copy-start | bytes 1769476
  27.3 15.2 %copy-start.1 = (s32[512]{0:T(512)S(1)}, s32[512]{0:T(512)}, u32[]{:S(2)}) copy-start(s32[512]{0:T(512)} %param.15) | copy-start | bytes 6148
  29.9 12.5 %all-to-all-start.1 = ((bf16[32,16,192]{2,1,0:T(8,128)(2,1)}), bf16[32,16,192]{2,1,0:T(8,128)(2,1)S(1)}, u32[]{:S(2)}, u32[]{:S(2)}) async-start(bf16[32,16,192]{2,1,0:T(8,128)(2,1)} %broadcast_in_dim.34), calls=%async_computation.1 | async-start | bytes 524288 | tf_op jit(solution)/shard_map/all_to_all | solution.py:26
  43.6 16.5 %all-to-all-start.2 = ((f32[8,16,192]{2,1,0:T(8,128)}), f32[8,16,192]{2,1,0:T(8,128)S(1)}, u32[]{:S(2)}, u32[]{:S(2)}) async-start(f32[8,16,192]{2,1,0:T(8,128)} %convolution_bitcast_fusion), calls=%async_computation.2 | async-start | bytes 262144 | tf_op jit(solution)/shard_map/all_to_all | solution.py:96

commit v9 on v8

--- a/solution.py
+++ b/solution.py
@@ -80,17 +80,22 @@
         "sgjpt,pgdt->sgjd", rounded, cache_pages[:, 1], preferred_element_type=jnp.float32
     )
     numerator = numerator + own_rounded[..., None] * own_value.astype(jnp.float32)[:, :, None, :]
-    context = (numerator / denominator[..., None]).astype(jnp.bfloat16).reshape(slot_count, -1)
-    gathered = exchange(context, "req")
+    context = (
+        jnp.broadcast_to(numerator[None], (req_count,) + numerator.shape)
+        / denominator[None, ..., None]
+    ).astype(jnp.bfloat16)
+    gathered = lax.all_to_all(context, "req", 0, 0).reshape((-1,) + numerator.shape[1:])
     wanted = first_slot + slot_ids
     selector = (occupant[None, :] == wanted[:, None]).astype(jnp.bfloat16)
-    attended = jnp.dot(selector, gathered, preferred_element_type=jnp.float32).astype(jnp.bfloat16)
+    attended = jnp.einsum(
+        "rn,ngjd->rgjd", selector, gathered, preferred_element_type=jnp.float32
+    ).astype(jnp.bfloat16)
     kv_count = lax.axis_size("kv")
     col_share = w_out.shape[0] // kv_count
     blocks = jnp.einsum(
-        "sa,kca->ksc",
+        "sgjd,kcgjd->ksc",
         attended,
-        w_out.reshape(kv_count, col_share, w_out.shape[1]),
+        w_out.reshape((kv_count, col_share) + numerator.shape[1:]),
         preferred_element_type=jnp.float32,
     )
     summed = jnp.sum(lax.all_to_all(blocks, "kv", 0, 0), axis=0)

time: 61.3 us -> 61.3 us (level)
  other arithmetic: 7.48 us -> 8.29 us
    convert_element_type x0 -> x2, other arithmetic: none -> 1.96 us  [the longest x1 1.14 us: per_device(): rounded = lax.optimization_barrier(weights.astype(jnp.bfloat16))]
    reduce_sum x1 -> x0, other arithmetic: 1.14 us -> none  [per_device(): denominator = jnp.sum(weights, axis=(-2, -1)) + own_weight]
    broadcast_in_dim x2 -> x0, local copies, waits for them, and re-layouts: 0.8 us -> none  [exchange(): sent = jnp.broadcast_to(rows[None], (count,) + rows.shape)]
where the time goes in v9:
time: 61.3 us; the launch traced here: 60.7 us
  waiting for transfers between devices  21.2 us (35%)
  starting transfers between devices  20.4 us (33%)
  other arithmetic  8.29 us (14%)
  matrix products  6.34 us (10%)
  Pallas kernels  2.42 us (4%)
  local copies, waits for them, and re-layouts  1.87 us (3%)
    all_to_all x1, starting transfers between devices, per_device(): lax.all_to_all(sent_rows, 'req', 0, 0).reshape(-1, w_qkv.shape[1])  8.58 us
    all_to_all x1, waiting for transfers between devices, per_device(): lax.all_to_all(context, 'req', 0, 0).reshape((-1,) + numerator.shape[1:])  8.23 us
    all_to_all x1, starting transfers between devices, per_device(): summed = jnp.sum(lax.all_to_all(blocks, 'kv', 0, 0), axis=0)  8.19 us
    all_to_all x1, waiting for transfers between devices, per_device(): summed = jnp.sum(lax.all_to_all(blocks, 'kv', 0, 0), axis=0)  7.51 us
    all_to_all x1, waiting for transfers between devices, per_device(): lax.all_to_all(sent_rows, 'req', 0, 0).reshape(-1, w_qkv.shape[1])  5.51 us
    all_to_all x1, starting transfers between devices, per_device(): lax.all_to_all(context, 'req', 0, 0).reshape((-1,) + numerator.shape[1:])  3.66 us
    dot_general x1, matrix products, per_device(): jnp.einsum('sgjd,pgdt->sgjpt', queries, cache_pages[:, 0], preferred_elem...  3.36 us
    pallas_call x1, Pallas kernels, per_device(): pl.pallas_call(_project_kernel, out_shape=jax.ShapeDtypeStruct((req_count...  2.42 us
  transfers between devices with their start and end apart: 3, of which 3 were waited for; matrix products, arithmetic and copies ran while one was open for 10% of the time, Pallas kernels for 0%

profile of v9, /device:TPU:1, one launch (start us, length us, event | category | flops | bytes accessed | tf_op | source)
XLA Modules:
  0.0 60.7 jit_solution(2172754819834209660)
XLA Ops:
  0.0 2.4 %shard_map.82 = bf16[32,16,384]{2,1,0:T(8,128)(2,1)} custom-call(bf16[16,1536]{1,0:T(8,128)(2,1)} %x_ref.1, f32[1536]{0:T(1024)} %g_ref.1, bf16[1536,384]{1,0:T(8,128)(2,1)} %w_ref.1), custom_call_target="tpu_custom_call" | custom-call | tf_op jit(solution)/shard_map/pallas_call | solution.py:38
  2.4 8.6 %all-to-all-start = ((bf16[32,16,384]{2,1,0:T(8,128)(2,1)}), bf16[32,16,384]{2,1,0:T(8,128)(2,1)S(1)}, u32[]{:S(2)}, u32[]{:S(2)}) async-start(bf16[32,16,384]{2,1,0:T(8,128)(2,1)} %shard_map.82), calls=%async_computation | async-start | bytes 786432 | tf_op jit(solution)/shard_map/all_to_all | solution.py:42
  11.0 0.7 %and_select_fusion = s32[16]{0:T(128)S(1)} fusion(s32[16]{0:T(128)} %param.13), kind=kLoop, calls=%fused_computation.48 | loop fusion | flops 256 | bytes 128 | tf_op jit(solution)/shard_map/jit(floor_divide)/jit(_where)/select_n | solution.py:49
  11.7 0.1 iota_compare_fusion.2
  11.8 1.7 %select_reduce_fusion = (s32[192]{0:T(256)S(1)}, s32[16,192]{1,0:T(8,128)S(1)}) fusion(s32[16,128]{1,0:T(8,128)} %param.14, pred[16,128]{1,0:T(8,128)(4,1)S(1)} %iota_compare_fusion.2), kind=kLoop, calls=%fused_computation.13 | loop fusion | flops 2356032 | bytes 23296 | tf_op jit(solution)/shard_map/reduce_sum | solution.py:57
  13.4 0.7 %multiply_reduce_fusion.2 = (s32[192]{0:T(256)S(1)}, s32[192]{0:T(256)S(1)}) fusion(s32[16,192]{1,0:T(8,128)S(1)} %get-tuple-element.8, s32[16]{0:T(128)} %param.13), kind=kLoop, calls=%fused_computation.34 | loop fusion | flops 11904 | bytes 13888 | tf_op jit(solution)/shard_map/reduce_sum | solution.py:56
  14.2 0.1 iota_compare_fusion.1
  14.3 0.1 add_compare_fusion
  14.4 0.8 %compare_and_fusion = (pred[16]{0:T(512)(128)(4,1)S(1)}, s32[16]{0:T(128)S(1)}) fusion(s32[512]{0:T(512)} %param.15, s32[]{:T(128)S(6)} %select_n.32), kind=kLoop, calls=%fused_computation.47 | loop fusion | flops 96 | bytes 148 | tf_op jit(solution)/shard_map/jit(_take)/and | solution.py:43
  15.2 0.6 broadcast_and_fusion
  15.8 5.5 %all-to-all-done = bf16[32,16,384]{2,1,0:T(8,128)(2,1)S(1)} async-done(((bf16[32,16,384]{2,1,0:T(8,128)(2,1)}), bf16[32,16,384]{2,1,0:T(8,128)(2,1)S(1)}, u32[]{:S(2)}, u32[]{:S(2)}) %all-to-all-start) | async-done | bytes 393248 | tf_op jit(solution)/shard_map/all_to_all | solution.py:42
  21.3 0.6 gather_fusion
  21.9 0.1 gather.7
  22.0 0.1 copy_select_fusion
  22.1 0.1 multiply_reduce_fusion
  22.1 0.0 copy-start.2
  22.1 3.4 %fusion.8 = (f32[16,2]{0,1:T(2,128)S(1)}, f32[16,2,192,128]{3,0,2,1:T(8,128)S(1)}) fusion(pred[16,192,128]{2,0,1:T(8,128)(4,1)S(1)} %broadcast_and_fusion, bf16[192,2,1,96,128]{4,3,2,1,0:T(8,128)(2,1)} %param.12, bf16[16,1,4,96]{3,0,2,1:T(8,128)(2,1)S(1)} %copy_select_fusion), kind=kOutput, calls=%fused_computation.11 | convolution fusion | flops 153354208 | bytes 8265856 | tf_op jit(solution)/shard_map/sgjd,pgdt->sgjpt/dot_general | solution.py:63
  25.5 1.1 %fusion.7 = (bf16[16,1,2,192,128]{4,0,3,2,1:T(8,128)(2,1)S(1)}, f32[16,2]{0,1:T(2,128)S(1)}) fusion(f32[16,2,192,128]{3,0,2,1:T(8,128)S(1)} %get-tuple-element.16, f32[16,2]{0,1:T(2,128)S(1)} %multiply_maximum_fusion, pred[16,192,128]{2,0,1:T(8,128)(4,1)S(1)} %broadcast_and_fusion), kind=kLoop, calls=%fused_computation.10 | loop fusion | flops 3932128 | bytes 5112064 | tf_op jit(solution)/shard_map/convert_element_type | solution.py:75
  26.7 0.6 copy-done.2
  27.3 0.0 copy-start
  27.3 0.0 copy-start.1
  27.3 1.8 %fusion.21 = f32[16,2,96]{2,0,1:T(8,128)S(1)} fusion(bf16[192,2,1,96,128]{4,3,2,1,0:T(8,128)(2,1)S(1)} %copy-done.2, bf16[16,1,2,192,128]{4,0,3,2,1:T(8,128)(2,1)S(1)} %get-tuple-element.11, f32[16,96]{1,0:T(8,128)S(1)} %get-tuple-element.13, f32[16,2]{0,1:T(2,128)S(1)} %bitcast_convert_fusion), kind=kOutput, calls=%fused_computation.20 | convolution fusion | flops 151001088 | bytes 6312960 | tf_op jit(solution)/shard_map/sgjpt,pgdt->sgjd/dot_general | solution.py:79
  29.1 0.8 %divide_convert_fusion = bf16[32,16,1,2,96]{4,1,3,2,0:T(8,128)(2,1)} fusion(f32[16,2]{0,1:T(2,128)S(1)} %exponential_add_fusion, f32[16,2,96]{2,0,1:T(8,128)S(1)} %fusion.21), kind=kLoop, calls=%fused_computation.25 | loop fusion | flops 196608 | bytes 209024 | tf_op jit(solution)/shard_map/convert_element_type | solution.py:86
  29.9 3.7 %all-to-all-start.1 = ((bf16[32,16,1,2,96]{4,1,3,2,0:T(8,128)(2,1)}), bf16[32,16,1,2,96]{4,1,3,2,0:T(8,128)(2,1)S(1)}, u32[]{:S(2)}, u32[]{:S(2)}) async-start(bf16[32,16,1,2,96]{4,1,3,2,0:T(8,128)(2,1)} %divide_convert_fusion), calls=%async_computation.1 | async-start | bytes 524288 | tf_op jit(solution)/shard_map/all_to_all | solution.py:87
  33.6 0.0 copy-done
  33.6 0.6 reshape.242
  34.2 8.2 %all-to-all-done.1 = bf16[32,16,1,2,96]{4,1,3,2,0:T(8,128)(2,1)S(1)} async-done(((bf16[32,16,1,2,96]{4,1,3,2,0:T(8,128)(2,1)}), bf16[32,16,1,2,96]{4,1,3,2,0:T(8,128)(2,1)S(1)}, u32[]{:S(2)}, u32[]{:S(2)}) %all-to-all-start.1) | async-done | bytes 196640 | tf_op jit(solution)/shard_map/all_to_all | solution.py:87
  42.4 0.0 copy-done.1
  42.5 1.2 %convolution_bitcast_fusion = f32[8,16,192]{2,1,0:T(8,128)} fusion(bf16[8,192,2,96]{1,0,3,2:T(8,128)(2,1)S(1)} %reshape.242, bf16[512,2,96]{2,0,1:T(8,128)(2,1)S(1)} %bitcast.101, s32[512]{0:T(512)S(1)} %copy-done.1, s32[16]{0:T(128)S(1)} %iota_add_fusion), kind=kOutput, calls=%fused_computation.17 | convolution fusion | flops 12594176 | bytes 886848 | tf_op jit(solution)/shard_map/sgjd,kcgjd->ksc/dot_general | solution.py:95
  43.6 8.2 %all-to-all-start.2 = ((f32[8,16,192]{2,1,0:T(8,128)}), f32[8,16,192]{2,1,0:T(8,128)S(1)}, u32[]{:S(2)}, u32[]{:S(2)}) async-start(f32[8,16,192]{2,1,0:T(8,128)} %convolution_bitcast_fusion), calls=%async_computation.2 | async-start | bytes 262144 | tf_op jit(solution)/shard_map/all_to_all | solution.py:101
  51.8 0.8 %dynamic-slice_convert_fusion = f32[16,192]{1,0:T(8,128)S(1)} fusion(bf16[16,1536]{1,0:T(8,128)(2,1)} %x_ref.1, s32[]{:T(128)S(6)} %select_n.30), kind=kLoop, calls=%fused_computation.37 | loop fusion | flops 3072 | bytes 18436 | tf_op jit(solution)/shard_map/convert_element_type | solution.py:35
  52.6 7.5 %all-to-all-done.2 = f32[8,16,192]{2,1,0:T(8,128)S(1)} async-done(((f32[8,16,192]{2,1,0:T(8,128)}), f32[8,16,192]{2,1,0:T(8,128)S(1)}, u32[]{:S(2)}, u32[]{:S(2)}) %all-to-all-start.2) | async-done | bytes 98336 | tf_op jit(solution)/shard_map/all_to_all | solution.py:101
  60.1 0.6 add_convert_fusion
  (10 shorter events, 0.1 us)
Async XLA Ops:
  2.4 18.9 %all-to-all-start = ((bf16[32,16,384]{2,1,0:T(8,128)(2,1)}), bf16[32,16,384]{2,1,0:T(8,128)(2,1)S(1)}, u32[]{:S(2)}, u32[]{:S(2)}) async-start(bf16[32,16,384]{2,1,0:T(8,128)(2,1)} %shard_map.82), calls=%async_computation | async-start | bytes 786432 | tf_op jit(solution)/shard_map/all_to_all | solution.py:42
  22.1 5.1 %copy-start.2 = (bf16[192,2,1,96,128]{4,3,2,1,0:T(8,128)(2,1)S(1)}, bf16[192,2,1,96,128]{4,3,2,1,0:T(8,128)(2,1)}, u32[]{:S(2)}) copy-start(bf16[192,2,1,96,128]{4,3,2,1,0:T(8,128)(2,1)} %param.12) | copy-start | bytes 28311556
  27.3 6.3 %copy-start = (bf16[1536,192]{0,1:T(8,128)(2,1)S(1)}, bf16[1536,192]{0,1:T(8,128)(2,1)}, u32[]{:S(2)}) copy-start(bf16[1536,192]{0,1:T(8,128)(2,1)} %param.11) | copy-start | bytes 1769476
  27.3 15.2 %copy-start.1 = (s32[512]{0:T(512)S(1)}, s32[512]{0:T(512)}, u32[]{:S(2)}) copy-start(s32[512]{0:T(512)} %param.15) | copy-start | bytes 6148
  29.9 12.5 %all-to-all-start.1 = ((bf16[32,16,1,2,96]{4,1,3,2,0:T(8,128)(2,1)}), bf16[32,16,1,2,96]{4,1,3,2,0:T(8,128)(2,1)S(1)}, u32[]{:S(2)}, u32[]{:S(2)}) async-start(bf16[32,16,1,2,96]{4,1,3,2,0:T(8,128)(2,1)} %divide_convert_fusion), calls=%async_computation.1 | async-start | bytes 524288 | tf_op jit(solution)/shard_map/all_to_all | solution.py:87
  43.6 16.5 %all-to-all-start.2 = ((f32[8,16,192]{2,1,0:T(8,128)}), f32[8,16,192]{2,1,0:T(8,128)S(1)}, u32[]{:S(2)}, u32[]{:S(2)}) async-start(f32[8,16,192]{2,1,0:T(8,128)} %convolution_bitcast_fusion), calls=%async_computation.2 | async-start | bytes 262144 | tf_op jit(solution)/shard_map/all_to_all | solution.py:101

commit v10 on v9

--- a/solution.py
+++ b/solution.py
@@ -12,12 +12,14 @@
 GROUP = 2
 
 
-def _project_kernel(x_ref, g_ref, w_ref, o_ref):
+def _project_kernel(x_ref, g_ref, w_ref, occ_ref, own_ref, o_ref):
     wide = x_ref[...].astype(jnp.float32)
     scale = lax.rsqrt(jnp.mean(wide * wide, axis=1, keepdims=True) + 1e-05)
     normed = (wide * scale * g_ref[...]).astype(jnp.bfloat16)
     rows = jnp.dot(normed, w_ref[...], preferred_element_type=jnp.float32).astype(jnp.bfloat16)
-    o_ref[...] = jnp.broadcast_to(rows[None], o_ref.shape)
+    route = (occ_ref[...] == own_ref[...]).astype(jnp.bfloat16)
+    placed = jnp.dot(route, rows, preferred_element_type=jnp.float32).astype(jnp.bfloat16)
+    o_ref[...] = placed.reshape(o_ref.shape)
 
 
 def exchange(rows, axis):
@@ -33,14 +35,19 @@
     first_slot = lax.axis_index("req") * slot_count
     slot_ids = jnp.arange(slot_count, dtype=jnp.int32)
     hidden_wide = hidden.astype(jnp.float32)
-    served = lax.dynamic_slice_in_dim(occupant, first_slot, slot_count)
     req_count = lax.axis_size("req")
     sent_rows = pl.pallas_call(
         _project_kernel,
         out_shape=jax.ShapeDtypeStruct((req_count, slot_count, w_qkv.shape[1]), jnp.bfloat16),
-    )(hidden, norm_gain, w_qkv)
-    every_row = lax.all_to_all(sent_rows, "req", 0, 0).reshape(-1, w_qkv.shape[1])
-    slot_rows = jnp.take(every_row, served, axis=0)
+    )(
+        hidden,
+        norm_gain,
+        w_qkv,
+        occupant.reshape(-1, 1),
+        (first_slot + slot_ids).reshape(1, -1),
+    )
+    arrived = lax.all_to_all(sent_rows, "req", 0, 0)
+    slot_rows = jnp.sum(arrived.astype(jnp.float32), axis=0).astype(jnp.bfloat16)
     slot_rows = slot_rows.reshape(slot_count, kv_local, GROUP + 2, HD)
     queries = slot_rows[:, :, :GROUP]
     own_key = slot_rows[:, :, GROUP]

time: 61.3 us -> 63.1 us (1.029)
  local copies, waits for them, and re-layouts: 1.87 us -> 2.82 us
  waiting for transfers between devices: 21.2 us -> 22 us
    reshape x0 -> x2, local copies, waits for them, and re-layouts: none -> 1.61 us  [the longest x1 1.53 us: per_device(): occupant.reshape(-1, 1)]
    all_to_all x1, waiting for transfers between devices: 5.51 us -> 6.28 us  [per_device(): arrived = lax.all_to_all(sent_rows, 'req', 0, 0)]
    and x1 -> x0, other arithmetic: 0.77 us -> none  [per_device(): slot_rows = jnp.take(every_row, served, axis=0)]
    gather x2 -> x0, local copies, waits for them, and re-layouts: 0.68 us -> none  [per_device(): slot_rows = jnp.take(every_row, served, axis=0)]
  transfers between devices with their start and end apart: 3 -> 3, of which waited for: 3 -> 3; matrix products, arithmetic and copies ran while one was open for 10% -> 9% of each run, Pallas kernels for 0% -> 0%
where the time goes in v10:
time: 63.1 us; the launch traced here: 62.6 us
  waiting for transfers between devices  22 us (35%)
  starting transfers between devices  20.4 us (32%)
  other arithmetic  8.04 us (13%)
  matrix products  6.33 us (10%)
  local copies, waits for them, and re-layouts  2.82 us (4%)
  Pallas kernels  2.8 us (4%)
    all_to_all x1, starting transfers between devices, per_device(): arrived = lax.all_to_all(sent_rows, 'req', 0, 0)  8.58 us
    all_to_all x1, waiting for transfers between devices, per_device(): lax.all_to_all(context, 'req', 0, 0).reshape((-1,) + numerator.shape[1:])  8.23 us
    all_to_all x1, starting transfers between devices, per_device(): summed = jnp.sum(lax.all_to_all(blocks, 'kv', 0, 0), axis=0)  8.19 us
    all_to_all x1, waiting for transfers between devices, per_device(): summed = jnp.sum(lax.all_to_all(blocks, 'kv', 0, 0), axis=0)  7.51 us
    all_to_all x1, waiting for transfers between devices, per_device(): arrived = lax.all_to_all(sent_rows, 'req', 0, 0)  6.28 us
    all_to_all x1, starting transfers between devices, per_device(): lax.all_to_all(context, 'req', 0, 0).reshape((-1,) + numerator.shape[1:])  3.65 us
    dot_general x1, matrix products, per_device(): jnp.einsum('sgjd,pgdt->sgjpt', queries, cache_pages[:, 0], preferred_elem...  3.35 us
    pallas_call x1, Pallas kernels, per_device(): pl.pallas_call(_project_kernel, out_shape=jax.ShapeDtypeStruct((req_count...  2.8 us
  transfers between devices with their start and end apart: 3, of which 3 were waited for; matrix products, arithmetic and copies ran while one was open for 9% of the time, Pallas kernels for 0%

profile of v10, /device:TPU:1, one launch (start us, length us, event | category | flops | bytes accessed | tf_op | source)
XLA Modules:
  0.0 62.6 jit_solution(13345757657517631269)
XLA Ops:
  0.0 0.5 iota_add_fusion.own_ref
  0.5 1.5 %copy.33.occ_ref = s32[512,1]{1,0:T(8,128)} copy(s32[512,1]{0,1:T(1,128)} %bitcast.95) | data formatting | bytes 4096 | tf_op jit(solution)/shard_map/reshape | solution.py:46
  2.0 2.8 %shard_map.82 = bf16[32,16,384]{2,1,0:T(8,128)(2,1)} custom-call(bf16[16,1536]{1,0:T(8,128)(2,1)} %x_ref.1, f32[1536]{0:T(1024)} %g_ref.1, bf16[1536,384]{1,0:T(8,128)(2,1)} %w_ref.1, s32[512,1]{1,0:T(8,128)} %copy.33.occ_ref, s32[1,16]{1,0:T(1,128)} %iota_add_fusion.own_ref), custom_call_target="tpu_custom_call" | custom-call | tf_op jit(solution)/shard_map/pallas_call | solution.py:39
  4.8 8.6 %all-to-all-start = ((bf16[32,16,384]{2,1,0:T(8,128)(2,1)}), bf16[32,16,384]{2,1,0:T(8,128)(2,1)S(1)}, u32[]{:S(2)}, u32[]{:S(2)}) async-start(bf16[32,16,384]{2,1,0:T(8,128)(2,1)} %shard_map.82), calls=%async_computation | async-start | bytes 786432 | tf_op jit(solution)/shard_map/all_to_all | solution.py:49
  13.4 0.7 %and_select_fusion = s32[16]{0:T(128)S(1)} fusion(s32[16]{0:T(128)} %param.13), kind=kLoop, calls=%fused_computation.41 | loop fusion | flops 256 | bytes 128 | tf_op jit(solution)/shard_map/jit(floor_divide)/jit(_where)/select_n | solution.py:56
  14.1 0.1 iota_compare_fusion.2
  14.2 1.7 %select_reduce_fusion = (s32[192]{0:T(256)S(1)}, s32[16,192]{1,0:T(8,128)S(1)}) fusion(s32[16,128]{1,0:T(8,128)} %param.14, pred[16,128]{1,0:T(8,128)(4,1)S(1)} %iota_compare_fusion.2), kind=kLoop, calls=%fused_computation.12 | loop fusion | flops 2356032 | bytes 23296 | tf_op jit(solution)/shard_map/reduce_sum | solution.py:64
  15.8 0.7 %multiply_reduce_fusion.2 = (s32[192]{0:T(256)S(1)}, s32[192]{0:T(256)S(1)}) fusion(s32[16,192]{1,0:T(8,128)S(1)} %get-tuple-element.8, s32[16]{0:T(128)} %param.13), kind=kLoop, calls=%fused_computation.32 | loop fusion | flops 11904 | bytes 13888 | tf_op jit(solution)/shard_map/reduce_sum | solution.py:63
  16.6 0.1 add_compare_fusion
  16.7 0.1 iota_compare_fusion.1
  16.8 0.6 broadcast_and_fusion
  17.4 6.3 %all-to-all-done = bf16[32,16,384]{2,1,0:T(8,128)(2,1)S(1)} async-done(((bf16[32,16,384]{2,1,0:T(8,128)(2,1)}), bf16[32,16,384]{2,1,0:T(8,128)(2,1)S(1)}, u32[]{:S(2)}, u32[]{:S(2)}) %all-to-all-start) | async-done | bytes 393248 | tf_op jit(solution)/shard_map/all_to_all | solution.py:49
  23.7 0.1 reduce_sum.79
  23.8 0.1 reshape.227
  23.9 0.1 multiply_reduce_fusion
  24.0 0.0 copy-start.2
  24.0 3.4 %fusion.8 = (f32[16,2]{0,1:T(2,128)S(1)}, f32[16,2,192,128]{3,0,2,1:T(8,128)S(1)}) fusion(pred[16,192,128]{2,0,1:T(8,128)(4,1)S(1)} %broadcast_and_fusion, bf16[192,2,1,96,128]{4,3,2,1,0:T(8,128)(2,1)} %param.12, bf16[16,1,2,96]{3,2,0,1:T(2,128)(2,1)S(1)} %slice.20), kind=kOutput, calls=%fused_computation.10 | convolution fusion | flops 153354208 | bytes 8263808 | tf_op jit(solution)/shard_map/sgjd,pgdt->sgjpt/dot_general | solution.py:70
  27.4 1.1 %fusion.7 = (bf16[16,1,2,192,128]{4,0,3,2,1:T(8,128)(2,1)S(1)}, f32[16,2]{0,1:T(2,128)S(1)}) fusion(f32[16,2,192,128]{3,0,2,1:T(8,128)S(1)} %get-tuple-element.14, f32[16,2]{0,1:T(2,128)S(1)} %multiply_maximum_fusion, pred[16,192,128]{2,0,1:T(8,128)(4,1)S(1)} %broadcast_and_fusion), kind=kLoop, calls=%fused_computation.9 | loop fusion | flops 3932128 | bytes 5112064 | tf_op jit(solution)/shard_map/convert_element_type | solution.py:82
  28.5 0.6 copy-done.2
  29.1 0.0 copy-start
  29.1 0.0 copy-start.1
  29.1 1.8 %fusion.21 = f32[16,2,96]{2,0,1:T(8,128)S(1)} fusion(bf16[192,2,1,96,128]{4,3,2,1,0:T(8,128)(2,1)S(1)} %copy-done.2, bf16[16,1,2,192,128]{4,0,3,2,1:T(8,128)(2,1)S(1)} %get-tuple-element.9, f32[16,96]{1,0:T(8,128)S(1)} %bitcast.96, f32[16,2]{0,1:T(2,128)S(1)} %bitcast_convert_fusion), kind=kOutput, calls=%fused_computation.19 | convolution fusion | flops 151001088 | bytes 6312960 | tf_op jit(solution)/shard_map/sgjpt,pgdt->sgjd/dot_general | solution.py:86
  30.9 0.8 %divide_convert_fusion = bf16[32,16,1,2,96]{4,1,3,2,0:T(8,128)(2,1)} fusion(f32[16,2]{0,1:T(2,128)S(1)} %exponential_add_fusion, f32[16,2,96]{2,0,1:T(8,128)S(1)} %fusion.21), kind=kLoop, calls=%fused_computation.24 | loop fusion | flops 196608 | bytes 209024 | tf_op jit(solution)/shard_map/convert_element_type | solution.py:93
  31.7 3.7 %all-to-all-start.1 = ((bf16[32,16,1,2,96]{4,1,3,2,0:T(8,128)(2,1)}), bf16[32,16,1,2,96]{4,1,3,2,0:T(8,128)(2,1)S(1)}, u32[]{:S(2)}, u32[]{:S(2)}) async-start(bf16[32,16,1,2,96]{4,1,3,2,0:T(8,128)(2,1)} %divide_convert_fusion), calls=%async_computation.1 | async-start | bytes 524288 | tf_op jit(solution)/shard_map/all_to_all | solution.py:94
  35.4 0.0 copy-done
  35.4 0.6 reshape.233
  36.0 8.2 %all-to-all-done.1 = bf16[32,16,1,2,96]{4,1,3,2,0:T(8,128)(2,1)S(1)} async-done(((bf16[32,16,1,2,96]{4,1,3,2,0:T(8,128)(2,1)}), bf16[32,16,1,2,96]{4,1,3,2,0:T(8,128)(2,1)S(1)}, u32[]{:S(2)}, u32[]{:S(2)}) %all-to-all-start.1) | async-done | bytes 196640 | tf_op jit(solution)/shard_map/all_to_all | solution.py:94
  44.3 0.0 copy-done.1
  44.3 1.2 %convolution_bitcast_fusion = f32[8,16,192]{2,1,0:T(8,128)} fusion(bf16[8,192,2,96]{1,0,3,2:T(8,128)(2,1)S(1)} %reshape.233, bf16[512,2,96]{2,0,1:T(8,128)(2,1)S(1)} %bitcast.93, s32[512]{0:T(512)S(1)} %copy-done.1, s32[16]{0:T(128)S(1)} %iota_add_fusion.1), kind=kOutput, calls=%fused_computation.16 | convolution fusion | flops 12594176 | bytes 886848 | tf_op jit(solution)/shard_map/sgjd,kcgjd->ksc/dot_general | solution.py:102
  45.5 8.2 %all-to-all-start.2 = ((f32[8,16,192]{2,1,0:T(8,128)}), f32[8,16,192]{2,1,0:T(8,128)S(1)}, u32[]{:S(2)}, u32[]{:S(2)}) async-start(f32[8,16,192]{2,1,0:T(8,128)} %convolution_bitcast_fusion), calls=%async_computation.2 | async-start | bytes 262144 | tf_op jit(solution)/shard_map/all_to_all | solution.py:108
  53.7 0.8 %dynamic-slice_convert_fusion = f32[16,192]{1,0:T(8,128)S(1)} fusion(bf16[16,1536]{1,0:T(8,128)(2,1)} %x_ref.1, s32[]{:T(128)S(6)} %select_n.12), kind=kLoop, calls=%fused_computation.37 | loop fusion | flops 3072 | bytes 18436 | tf_op jit(solution)/shard_map/convert_element_type | solution.py:37
  54.4 7.5 %all-to-all-done.2 = f32[8,16,192]{2,1,0:T(8,128)S(1)} async-done(((f32[8,16,192]{2,1,0:T(8,128)}), f32[8,16,192]{2,1,0:T(8,128)S(1)}, u32[]{:S(2)}, u32[]{:S(2)}) %all-to-all-start.2) | async-done | bytes 98336 | tf_op jit(solution)/shard_map/all_to_all | solution.py:108
  62.0 0.6 add_convert_fusion
  (10 shorter events, 0.1 us)
Async XLA Ops:
  4.8 18.9 %all-to-all-start = ((bf16[32,16,384]{2,1,0:T(8,128)(2,1)}), bf16[32,16,384]{2,1,0:T(8,128)(2,1)S(1)}, u32[]{:S(2)}, u32[]{:S(2)}) async-start(bf16[32,16,384]{2,1,0:T(8,128)(2,1)} %shard_map.82), calls=%async_computation | async-start | bytes 786432 | tf_op jit(solution)/shard_map/all_to_all | solution.py:49
  24.0 5.1 %copy-start.2 = (bf16[192,2,1,96,128]{4,3,2,1,0:T(8,128)(2,1)S(1)}, bf16[192,2,1,96,128]{4,3,2,1,0:T(8,128)(2,1)}, u32[]{:S(2)}) copy-start(bf16[192,2,1,96,128]{4,3,2,1,0:T(8,128)(2,1)} %param.12) | copy-start | bytes 28311556
  29.1 6.3 %copy-start = (bf16[1536,192]{0,1:T(8,128)(2,1)S(1)}, bf16[1536,192]{0,1:T(8,128)(2,1)}, u32[]{:S(2)}) copy-start(bf16[1536,192]{0,1:T(8,128)(2,1)} %param.11) | copy-start | bytes 1769476
  29.1 15.2 %copy-start.1 = (s32[512]{0:T(512)S(1)}, s32[512]{0:T(512)}, u32[]{:S(2)}) copy-start(s32[512]{0:T(512)} %param.15) | copy-start | bytes 6148
  31.7 12.5 %all-to-all-start.1 = ((bf16[32,16,1,2,96]{4,1,3,2,0:T(8,128)(2,1)}), bf16[32,16,1,2,96]{4,1,3,2,0:T(8,128)(2,1)S(1)}, u32[]{:S(2)}, u32[]{:S(2)}) async-start(bf16[32,16,1,2,96]{4,1,3,2,0:T(8,128)(2,1)} %divide_convert_fusion), calls=%async_computation.1 | async-start | bytes 524288 | tf_op jit(solution)/shard_map/all_to_all | solution.py:94
  45.5 16.5 %all-to-all-start.2 = ((f32[8,16,192]{2,1,0:T(8,128)}), f32[8,16,192]{2,1,0:T(8,128)S(1)}, u32[]{:S(2)}, u32[]{:S(2)}) async-start(f32[8,16,192]{2,1,0:T(8,128)} %convolution_bitcast_fusion), calls=%async_computation.2 | async-start | bytes 262144 | tf_op jit(solution)/shard_map/all_to_all | solution.py:108

commit v11 on v9

--- a/solution.py
+++ b/solution.py
@@ -40,7 +40,10 @@
         out_shape=jax.ShapeDtypeStruct((req_count, slot_count, w_qkv.shape[1]), jnp.bfloat16),
     )(hidden, norm_gain, w_qkv)
     every_row = lax.all_to_all(sent_rows, "req", 0, 0).reshape(-1, w_qkv.shape[1])
-    slot_rows = jnp.take(every_row, served, axis=0)
+    picker = (served[:, None] == jnp.arange(every_row.shape[0], dtype=jnp.int32)[None, :])
+    slot_rows = jnp.dot(
+        picker.astype(jnp.bfloat16), every_row, preferred_element_type=jnp.float32
+    ).astype(jnp.bfloat16)
     slot_rows = slot_rows.reshape(slot_count, kv_local, GROUP + 2, HD)
     queries = slot_rows[:, :, :GROUP]
     own_key = slot_rows[:, :, GROUP]

time: 61.3 us -> 61 us (level)
  other arithmetic: 8.29 us -> 7.53 us
    and x1 -> x0, other arithmetic: 0.77 us -> none  [per_device(): slot_rows = jnp.take(every_row, served, axis=0)]
    dynamic_slice x0 -> x1, local copies, waits for them, and re-layouts: none -> 0.76 us  [per_device(): served = lax.dynamic_slice_in_dim(occupant, first_slot, slot_count)]
    gather x2 -> x0, local copies, waits for them, and re-layouts: 0.68 us -> none  [per_device(): slot_rows = jnp.take(every_row, served, axis=0)]
where the time goes in v11:
time: 61 us; the launch traced here: 60.5 us
  waiting for transfers between devices  21.3 us (35%)
  starting transfers between devices  20.4 us (33%)
  other arithmetic  7.53 us (12%)
  matrix products  6.53 us (11%)
  Pallas kernels  2.42 us (4%)
  local copies, waits for them, and re-layouts  2.18 us (4%)
    all_to_all x1, starting transfers between devices, per_device(): lax.all_to_all(sent_rows, 'req', 0, 0).reshape(-1, w_qkv.shape[1])  8.58 us
    all_to_all x1, waiting for transfers between devices, per_device(): lax.all_to_all(context, 'req', 0, 0).reshape((-1,) + numerator.shape[1:])  8.23 us
    all_to_all x1, starting transfers between devices, per_device(): summed = jnp.sum(lax.all_to_all(blocks, 'kv', 0, 0), axis=0)  8.19 us
    all_to_all x1, waiting for transfers between devices, per_device(): summed = jnp.sum(lax.all_to_all(blocks, 'kv', 0, 0), axis=0)  7.51 us
    all_to_all x1, waiting for transfers between devices, per_device(): lax.all_to_all(sent_rows, 'req', 0, 0).reshape(-1, w_qkv.shape[1])  5.52 us
    all_to_all x1, starting transfers between devices, per_device(): lax.all_to_all(context, 'req', 0, 0).reshape((-1,) + numerator.shape[1:])  3.65 us
    dot_general x1, matrix products, per_device(): jnp.einsum('sgjd,pgdt->sgjpt', queries, cache_pages[:, 0], preferred_elem...  3.35 us
    pallas_call x1, Pallas kernels, per_device(): pl.pallas_call(_project_kernel, out_shape=jax.ShapeDtypeStruct((req_count...  2.42 us
  transfers between devices with their start and end apart: 3, of which 3 were waited for; matrix products, arithmetic and copies ran while one was open for 10% of the time, Pallas kernels for 0%

profile of v11, /device:TPU:1, one launch (start us, length us, event | category | flops | bytes accessed | tf_op | source)
XLA Modules:
  0.0 60.5 jit_solution(13899258698170759892)
XLA Ops:
  0.0 2.4 %shard_map.82 = bf16[32,16,384]{2,1,0:T(8,128)(2,1)} custom-call(bf16[16,1536]{1,0:T(8,128)(2,1)} %x_ref.1, f32[1536]{0:T(1024)} %g_ref.1, bf16[1536,384]{1,0:T(8,128)(2,1)} %w_ref.1), custom_call_target="tpu_custom_call" | custom-call | tf_op jit(solution)/shard_map/pallas_call | solution.py:38
  2.4 8.6 %all-to-all-start = ((bf16[32,16,384]{2,1,0:T(8,128)(2,1)}), bf16[32,16,384]{2,1,0:T(8,128)(2,1)S(1)}, u32[]{:S(2)}, u32[]{:S(2)}) async-start(bf16[32,16,384]{2,1,0:T(8,128)(2,1)} %shard_map.82), calls=%async_computation | async-start | bytes 786432 | tf_op jit(solution)/shard_map/all_to_all | solution.py:42
  11.0 0.7 %and_select_fusion = s32[16]{0:T(128)S(1)} fusion(s32[16]{0:T(128)} %param.13), kind=kLoop, calls=%fused_computation.45 | loop fusion | flops 256 | bytes 128 | tf_op jit(solution)/shard_map/jit(floor_divide)/jit(_where)/select_n | solution.py:52
  11.7 0.1 iota_compare_fusion.4
  11.8 1.7 %select_reduce_fusion = (s32[192]{0:T(256)S(1)}, s32[16,192]{1,0:T(8,128)S(1)}) fusion(s32[16,128]{1,0:T(8,128)} %param.14, pred[16,128]{1,0:T(8,128)(4,1)S(1)} %iota_compare_fusion.4), kind=kLoop, calls=%fused_computation.12 | loop fusion | flops 2356032 | bytes 23296 | tf_op jit(solution)/shard_map/reduce_sum | solution.py:60
  13.4 0.7 %multiply_reduce_fusion.2 = (s32[192]{0:T(256)S(1)}, s32[192]{0:T(256)S(1)}) fusion(s32[16,192]{1,0:T(8,128)S(1)} %get-tuple-element.8, s32[16]{0:T(128)} %param.13), kind=kLoop, calls=%fused_computation.36 | loop fusion | flops 11904 | bytes 13888 | tf_op jit(solution)/shard_map/reduce_sum | solution.py:59
  14.2 0.8 %dynamic_slice.7 = s32[16]{0:T(128)S(1)} dynamic-slice(s32[512]{0:T(512)} %param.15, s32[]{:T(128)S(6)} %select_n.17), dynamic_slice_sizes={16} | dynamic-slice | bytes 132 | tf_op jit(solution)/shard_map/dynamic_slice | solution.py:36
  14.9 0.1 add_compare_fusion
  15.1 0.1 iota_compare_fusion.1
  15.2 0.6 broadcast_and_fusion
  15.8 5.5 %all-to-all-done = bf16[32,16,384]{2,1,0:T(8,128)(2,1)S(1)} async-done(((bf16[32,16,384]{2,1,0:T(8,128)(2,1)}), bf16[32,16,384]{2,1,0:T(8,128)(2,1)S(1)}, u32[]{:S(2)}, u32[]{:S(2)}) %all-to-all-start) | async-done | bytes 393248 | tf_op jit(solution)/shard_map/all_to_all | solution.py:42
  21.3 0.2 convolution_convert_fusion
  21.5 0.1 reshape.220
  21.6 0.1 multiply_reduce_fusion
  21.7 0.0 copy-start.2
  21.7 3.4 %fusion.8 = (f32[16,2]{0,1:T(2,128)S(1)}, f32[16,2,192,128]{3,0,2,1:T(8,128)S(1)}) fusion(pred[16,192,128]{2,0,1:T(8,128)(4,1)S(1)} %broadcast_and_fusion, bf16[192,2,1,96,128]{4,3,2,1,0:T(8,128)(2,1)} %param.12, bf16[16,1,2,96]{3,2,0,1:T(2,128)(2,1)S(1)} %slice.20), kind=kOutput, calls=%fused_computation.10 | convolution fusion | flops 153354208 | bytes 8263808 | tf_op jit(solution)/shard_map/sgjd,pgdt->sgjpt/dot_general | solution.py:66
  25.1 1.1 %fusion.7 = (bf16[16,1,2,192,128]{4,0,3,2,1:T(8,128)(2,1)S(1)}, f32[16,2]{0,1:T(2,128)S(1)}) fusion(f32[16,2,192,128]{3,0,2,1:T(8,128)S(1)} %get-tuple-element.14, f32[16,2]{0,1:T(2,128)S(1)} %multiply_maximum_fusion, pred[16,192,128]{2,0,1:T(8,128)(4,1)S(1)} %broadcast_and_fusion), kind=kLoop, calls=%fused_computation.9 | loop fusion | flops 3932128 | bytes 5112064 | tf_op jit(solution)/shard_map/convert_element_type | solution.py:78
  26.2 0.6 %copy-done.2 = bf16[192,2,1,96,128]{4,3,2,1,0:T(8,128)(2,1)S(1)} copy-done((bf16[192,2,1,96,128]{4,3,2,1,0:T(8,128)(2,1)S(1)}, bf16[192,2,1,96,128]{4,3,2,1,0:T(8,128)(2,1)}, u32[]{:S(2)}) %copy-start.2) | copy-done | bytes 9437208
  26.8 0.0 copy-start
  26.8 0.0 copy-start.1
  26.8 1.8 %fusion.21 = f32[16,2,96]{2,0,1:T(8,128)S(1)} fusion(bf16[192,2,1,96,128]{4,3,2,1,0:T(8,128)(2,1)S(1)} %copy-done.2, bf16[16,1,2,192,128]{4,0,3,2,1:T(8,128)(2,1)S(1)} %get-tuple-element.9, f32[16,96]{1,0:T(8,128)S(1)} %bitcast.96, f32[16,2]{0,1:T(2,128)S(1)} %bitcast_convert_fusion), kind=kOutput, calls=%fused_computation.20 | convolution fusion | flops 151001088 | bytes 6312960 | tf_op jit(solution)/shard_map/sgjpt,pgdt->sgjd/dot_general | solution.py:82
  28.7 0.1 copy.19
  28.8 0.9 %divide_convert_fusion = bf16[32,16,1,2,96]{4,3,2,1,0:T(2,128)(2,1)} fusion(f32[16,2]{1,0:T(8,128)S(1)} %copy.19, f32[16,2,96]{2,1,0:T(2,128)S(1)} %copy.18), kind=kLoop, calls=%fused_computation.25 | loop fusion | flops 196608 | bytes 209024 | tf_op jit(solution)/shard_map/convert_element_type | solution.py:89
  29.7 3.7 %all-to-all-start.1 = ((bf16[32,16,1,2,96]{4,3,2,1,0:T(2,128)(2,1)}), bf16[32,16,1,2,96]{4,3,2,1,0:T(2,128)(2,1)S(1)}, u32[]{:S(2)}, u32[]{:S(2)}) async-start(bf16[32,16,1,2,96]{4,3,2,1,0:T(2,128)(2,1)} %divide_convert_fusion), calls=%async_computation.1 | async-start | bytes 524288 | tf_op jit(solution)/shard_map/all_to_all | solution.py:90
  33.3 0.0 copy-done
  33.4 0.6 reshape.226
  34.0 8.2 %all-to-all-done.1 = bf16[32,16,1,2,96]{4,3,2,1,0:T(2,128)(2,1)S(1)} async-done(((bf16[32,16,1,2,96]{4,3,2,1,0:T(2,128)(2,1)}), bf16[32,16,1,2,96]{4,3,2,1,0:T(2,128)(2,1)S(1)}, u32[]{:S(2)}, u32[]{:S(2)}) %all-to-all-start.1) | async-done | bytes 196640 | tf_op jit(solution)/shard_map/all_to_all | solution.py:90
  42.2 0.0 copy-done.1
  42.2 1.2 %convolution_bitcast_fusion = f32[8,16,192]{2,1,0:T(8,128)} fusion(bf16[8,192,2,96]{1,0,3,2:T(8,128)(2,1)S(1)} %reshape.226, bf16[512,2,96]{2,1,0:T(2,128)(2,1)S(1)} %bitcast.94, s32[512]{0:T(512)S(1)} %copy-done.1, s32[16]{0:T(128)S(1)} %iota_add_fusion), kind=kOutput, calls=%fused_computation.16 | convolution fusion | flops 12594176 | bytes 886848 | tf_op jit(solution)/shard_map/sgjd,kcgjd->ksc/dot_general | solution.py:98
  43.4 8.2 %all-to-all-start.2 = ((f32[8,16,192]{2,1,0:T(8,128)}), f32[8,16,192]{2,1,0:T(8,128)S(1)}, u32[]{:S(2)}, u32[]{:S(2)}) async-start(f32[8,16,192]{2,1,0:T(8,128)} %convolution_bitcast_fusion), calls=%async_computation.2 | async-start | bytes 262144 | tf_op jit(solution)/shard_map/all_to_all | solution.py:104
  51.6 0.8 %dynamic-slice_convert_fusion = f32[16,192]{1,0:T(8,128)S(1)} fusion(bf16[16,1536]{1,0:T(8,128)(2,1)} %x_ref.1, s32[]{:T(128)S(6)} %select_n.15), kind=kLoop, calls=%fused_computation.41 | loop fusion | flops 3072 | bytes 18436 | tf_op jit(solution)/shard_map/convert_element_type | solution.py:35
  52.4 7.5 %all-to-all-done.2 = f32[8,16,192]{2,1,0:T(8,128)S(1)} async-done(((f32[8,16,192]{2,1,0:T(8,128)}), f32[8,16,192]{2,1,0:T(8,128)S(1)}, u32[]{:S(2)}, u32[]{:S(2)}) %all-to-all-start.2) | async-done | bytes 98336 | tf_op jit(solution)/shard_map/all_to_all | solution.py:104
  59.9 0.6 add_convert_fusion
  (10 shorter events, 0.1 us)
Async XLA Ops:
  2.4 18.9 %all-to-all-start = ((bf16[32,16,384]{2,1,0:T(8,128)(2,1)}), bf16[32,16,384]{2,1,0:T(8,128)(2,1)S(1)}, u32[]{:S(2)}, u32[]{:S(2)}) async-start(bf16[32,16,384]{2,1,0:T(8,128)(2,1)} %shard_map.82), calls=%async_computation | async-start | bytes 786432 | tf_op jit(solution)/shard_map/all_to_all | solution.py:42
  21.7 5.1 %copy-start.2 = (bf16[192,2,1,96,128]{4,3,2,1,0:T(8,128)(2,1)S(1)}, bf16[192,2,1,96,128]{4,3,2,1,0:T(8,128)(2,1)}, u32[]{:S(2)}) copy-start(bf16[192,2,1,96,128]{4,3,2,1,0:T(8,128)(2,1)} %param.12) | copy-start | bytes 28311556
  26.8 6.5 %copy-start = (bf16[1536,192]{0,1:T(8,128)(2,1)S(1)}, bf16[1536,192]{0,1:T(8,128)(2,1)}, u32[]{:S(2)}) copy-start(bf16[1536,192]{0,1:T(8,128)(2,1)} %param.11) | copy-start | bytes 1769476
  26.8 15.4 %copy-start.1 = (s32[512]{0:T(512)S(1)}, s32[512]{0:T(512)}, u32[]{:S(2)}) copy-start(s32[512]{0:T(512)} %param.15) | copy-start | bytes 6148
  29.7 12.5 %all-to-all-start.1 = ((bf16[32,16,1,2,96]{4,3,2,1,0:T(2,128)(2,1)}), bf16[32,16,1,2,96]{4,3,2,1,0:T(2,128)(2,1)S(1)}, u32[]{:S(2)}, u32[]{:S(2)}) async-start(bf16[32,16,1,2,96]{4,3,2,1,0:T(2,128)(2,1)} %divide_convert_fusion), calls=%async_computation.1 | async-start | bytes 524288 | tf_op jit(solution)/shard_map/all_to_all | solution.py:90
  43.4 16.5 %all-to-all-start.2 = ((f32[8,16,192]{2,1,0:T(8,128)}), f32[8,16,192]{2,1,0:T(8,128)S(1)}, u32[]{:S(2)}, u32[]{:S(2)}) async-start(f32[8,16,192]{2,1,0:T(8,128)} %convolution_bitcast_fusion), calls=%async_computation.2 | async-start | bytes 262144 | tf_op jit(solution)/shard_map/all_to_all | solution.py:104
